TPU v7x, 32 devices: a whole 2x2x4 slice. The times are simulated.
32 devices in a mesh: groups: 2 (over x), ctx: 8 (over z, y), dp: 2 (over core).
Axes of the slice: x: 2, y: 2, z: 4, core: 2. Of those that a mesh axis runs over, the one named last changes fastest.
Arguments:
- hidden_in: bfloat16 [4, 2048, 4608], P(('groups', 'dp'), 'ctx'), parts along dimension 0, may hold values from -6 to 6
- norm_gain: float32 [4608], replicated, may hold values from 0.1 to 1.9
- key_weight: bfloat16 [4608, 1024], P(('ctx', 'dp')), may hold values from -0.09375 to 0.09375
- value_weight: bfloat16 [4608, 1024], P(('ctx', 'dp')), may hold values from -0.09375 to 0.09375
- queries: bfloat16 [4, 2048, 2048], P(('groups', 'dp'), 'ctx'), parts along dimension 0, may hold values from -64 to 64
- out_grad: bfloat16 [4, 2048, 2048], P(('groups', 'dp'), 'ctx'), parts along dimension 0, may hold values from -96 to 96
Outputs:
- hidden_grad: bfloat16 [4, 2048, 4608], P(('groups', 'dp'), 'ctx'), parts along dimension 0
- query_gradient: bfloat16 [4, 2048, 2048], P(('groups', 'dp'), 'ctx'), parts along dimension 0
- key_weight_grad: float32 [9216, 1024], P(('groups', 'ctx', 'dp')), parts along dimension 0
- value_weight_grad: float32 [9216, 1024], P(('groups', 'ctx', 'dp')), parts along dimension 0
- gain_grad: float32 [9216], P(('groups', 'ctx', 'dp')), parts along dimension 0
There are 2 independent parts, one for each index of `groups`. A program takes and returns all parts, laid end to end along the dimension named above; an argument that names none is the same for every part. Nothing has to cross between parts.
All inputs are finite; a program needn't handle non-finite values.
Results may differ from a plain program's by a relative error of at most 0.023.
The roundings to bfloat16 on the way count: a program that leaves them out, or rounds other values in their place, can miss the bound.
Values may be sent and summed in bfloat16 or wider, within the bound.
No kernel may reach another device: no remote copies, remote signals or barrier semaphores. Data moves between devices by JAX's collectives and lax.ppermute only.
A program may use at most 192 MiB of HBM per device.

v0:
```python
import jax
import jax.numpy as jnp
from jax import lax
from jax.sharding import PartitionSpec as P

HEADS = 16
KV_HEADS = 8
HEAD_DIM = 128
WINDOW = 256


score_scale = 1.0 / 12.0
grad_scale = 1.0 / 64.0
norm_eps = 1e-06
rope_base = 10000.0
masked_score = -1e30


def from_behind(value, axis, steps):
    count = lax.axis_size(axis)
    initial, last = (max(0, -steps), min(count, count - steps))
    return lax.ppermute(value, axis, [(source, source + steps) for source in range(initial, last)])


def rotation(positions):
    half_dim = HEAD_DIM // 2
    frequency = rope_base ** (-jnp.arange(half_dim, dtype=jnp.float32) / half_dim)
    angles = positions.astype(jnp.float32)[:, None] * frequency[None, :]
    return (jnp.cos(angles)[:, None, :], jnp.sin(angles)[:, None, :])


def rotate(tensor, cosine_table, sine_table):
    half_dim = HEAD_DIM // 2
    front_half = tensor[..., :half_dim]
    back_half = tensor[..., half_dim:]
    return jnp.concatenate(
        [
            front_half * cosine_table - back_half * sine_table,
            back_half * cosine_table + front_half * sine_table,
        ],
        axis=-1,
    )


def rotate_back(tensor, cosine_table, sine_table):
    half_dim = HEAD_DIM // 2
    front_half = tensor[..., :half_dim]
    back_half = tensor[..., half_dim:]
    return jnp.concatenate(
        [
            front_half * cosine_table + back_half * sine_table,
            back_half * cosine_table - front_half * sine_table,
        ],
        axis=-1,
    )


def block_backward(
    query_block, grad_block, nearby_keys, near_values, distant_keys, far_values, has_prev
):
    tok_rows = query_block.shape[0]
    group_size = HEADS // KV_HEADS
    query_head_split = query_block.reshape(tok_rows, KV_HEADS, group_size, HEAD_DIM)
    gradient_heads = grad_block.reshape(tok_rows, KV_HEADS, group_size, HEAD_DIM)
    row_index = jnp.arange(tok_rows)[:, None]
    col_index = jnp.arange(tok_rows)[None, :]
    near_mask = (col_index <= row_index) & (row_index - col_index < WINDOW)
    far_mask = (col_index > row_index + tok_rows - WINDOW) & has_prev

    def pair_products(leftover_heads, key_row_block):
        return jnp.einsum(
            "qbak,wbk->baqw", leftover_heads, key_row_block, preferred_element_type=jnp.float32
        )

    near_scores = jnp.where(
        near_mask, pair_products(query_head_split, nearby_keys) * score_scale, masked_score
    )
    far_scores = jnp.where(
        far_mask, pair_products(query_head_split, distant_keys) * score_scale, masked_score
    )
    row_top = jnp.maximum(jnp.max(near_scores, -1), jnp.max(far_scores, -1))[..., None]
    near_exp = jnp.where(near_mask, jnp.exp(near_scores - row_top), 0.0)
    far_exp = jnp.where(far_mask, jnp.exp(far_scores - row_top), 0.0)
    row_total = (jnp.sum(near_exp, -1) + jnp.sum(far_exp, -1))[..., None]
    near_probs = near_exp / row_total
    far_probs = far_exp / row_total
    near_dprobs = pair_products(gradient_heads, near_values)
    far_dprobs = pair_products(gradient_heads, far_values)
    weighted = (jnp.sum(near_probs * near_dprobs, -1) + jnp.sum(far_probs * far_dprobs, -1))[
        ..., None
    ]
    nearby_score_gradient = (near_probs * (near_dprobs - weighted) * score_scale).astype(
        jnp.bfloat16
    )
    distant_score_gradient = (far_probs * (far_dprobs - weighted) * score_scale).astype(
        jnp.bfloat16
    )
    nearby_reduced = near_probs.astype(jnp.bfloat16)
    distant_reduced = far_probs.astype(jnp.bfloat16)
    query_gradient = jnp.einsum(
        "xqwc,cxi->wxqi", nearby_score_gradient, nearby_keys, preferred_element_type=jnp.float32
    )
    query_gradient = query_gradient + jnp.einsum(
        "xqwc,cxi->wxqi", distant_score_gradient, distant_keys, preferred_element_type=jnp.float32
    )
    nearby_key = jnp.einsum(
        "woia,iwon->awn",
        nearby_score_gradient,
        query_head_split,
        preferred_element_type=jnp.float32,
    )
    distant_key = jnp.einsum(
        "woia,iwon->awn",
        distant_score_gradient,
        query_head_split,
        preferred_element_type=jnp.float32,
    )
    nearby_value = jnp.einsum(
        "woia,iwon->awn", nearby_reduced, gradient_heads, preferred_element_type=jnp.float32
    )
    distant_value = jnp.einsum(
        "woia,iwon->awn", distant_reduced, gradient_heads, preferred_element_type=jnp.float32
    )
    query_out = query_gradient.reshape(tok_rows, HEADS * HEAD_DIM).astype(jnp.bfloat16)
    return (query_out, nearby_key, nearby_value, distant_key, distant_value)


def body(hidden_in, norm_gain, key_weight, value_weight, queries, out_grad):
    tok_rows = hidden_in.shape[1]
    key_width = key_weight.shape[1]
    inputs = hidden_in[0].astype(jnp.float32)
    inverse = lax.rsqrt(jnp.mean(inputs * inputs, axis=-1, keepdims=True) + norm_eps)
    normed = (inputs * inverse * norm_gain).astype(jnp.bfloat16)
    full_key, full_value = (
        lax.all_gather(key_weight, ("ctx", "dp"), axis=0, tiled=True),
        lax.all_gather(value_weight, ("ctx", "dp"), axis=0, tiled=True),
    )
    key_raw = jnp.dot(normed, full_key, preferred_element_type=jnp.float32)
    value_rows = jnp.dot(normed, full_value, preferred_element_type=jnp.float32).astype(
        jnp.bfloat16
    )
    ctx_index = lax.axis_index("ctx")
    positions = ctx_index * tok_rows + jnp.arange(tok_rows, dtype=jnp.int32)
    cosine_table, sine_table = rotation(positions)
    key_row_block = rotate(key_raw.reshape(tok_rows, KV_HEADS, HEAD_DIM), cosine_table, sine_table)
    key_row_block = key_row_block.astype(jnp.bfloat16).reshape(tok_rows, key_width)
    prev_key, prev_value = from_behind((key_row_block, value_rows), "ctx", 1)
    head_shape = (tok_rows, KV_HEADS, HEAD_DIM)
    query_gradient, nearby_key, nearby_value, distant_key, distant_value = block_backward(
        queries[0],
        out_grad[0],
        key_row_block.reshape(head_shape),
        value_rows.reshape(head_shape),
        prev_key.reshape(head_shape),
        prev_value.reshape(head_shape),
        ctx_index > 0,
    )
    incoming_key, incoming_value = from_behind(
        (distant_key.astype(jnp.bfloat16), distant_value.astype(jnp.bfloat16)), "ctx", -1
    )
    key_grad = nearby_key + incoming_key.astype(jnp.float32)
    value_grad = nearby_value + incoming_value.astype(jnp.float32)
    key_grad_raw = (
        rotate_back(key_grad, cosine_table, sine_table)
        .astype(jnp.bfloat16)
        .reshape(tok_rows, key_width)
    )
    value_low = value_grad.astype(jnp.bfloat16).reshape(tok_rows, key_width)
    key_part = jnp.einsum("td,tk->dk", normed, key_grad_raw, preferred_element_type=jnp.float32)
    value_part = jnp.einsum("td,tk->dk", normed, value_low, preferred_element_type=jnp.float32)
    stacked = lax.psum_scatter(
        (jnp.concatenate([key_part, value_part], axis=1) * grad_scale).astype(jnp.bfloat16),
        ("ctx", "dp"),
        scatter_dimension=0,
        tiled=True,
    ).astype(jnp.float32)
    key_weight_grad = stacked[:, :key_width]
    value_weight_grad = stacked[:, key_width:]
    normed_grad = jnp.einsum(
        "tk,dk->td", key_grad_raw, full_key, preferred_element_type=jnp.float32
    )
    normed_grad = normed_grad + jnp.einsum(
        "tk,dk->td", value_low, full_value, preferred_element_type=jnp.float32
    )
    scaled = normed_grad * norm_gain
    cubed = inverse * inverse * inverse
    hidden_grad = (
        inverse * scaled - inputs * cubed * jnp.mean(scaled * inputs, axis=-1, keepdims=True)
    ).astype(jnp.bfloat16)
    gain_term = jnp.sum(normed_grad * inputs * inverse, axis=0) * grad_scale
    gain_grad = lax.psum_scatter(gain_term, ("ctx", "dp"), scatter_dimension=0, tiled=True)
    return (hidden_grad[None], query_gradient[None], key_weight_grad, value_weight_grad, gain_grad)


def solution(mesh):
    return jax.shard_map(
        body,
        mesh=mesh,
        in_specs=(
            P(("groups", "dp"), "ctx", None),
            P(),
            P(("ctx", "dp"), None),
            P(("ctx", "dp"), None),
            P(("groups", "dp"), "ctx", None),
            P(("groups", "dp"), "ctx", None),
        ),
        out_specs=(
            P(("groups", "dp"), "ctx", None),
            P(("groups", "dp"), "ctx", None),
            P(("groups", "ctx", "dp"), None),
            P(("groups", "ctx", "dp"), None),
            P(("groups", "ctx", "dp")),
        ),
        check_vma=False,
    )
```

profile of v0, /device:TPU:0, one launch (start us, length us, event | category | flops | bytes accessed | tf_op | source)
XLA Modules:
  0.0 531.6 jit_solution(3950235308410985168)
XLA Ops:
  7.2 0.0 copy-start
  7.2 0.0 all-gather.5.cloned.1.call-start
  7.2 0.7 all-gather.5.cloned.1.call-update
  7.9 0.0 all-gather.3.cloned.1.call-start
  8.0 0.7 all-gather.3.cloned.1.call-update
  8.7 0.0 reduce-scatter.4.cloned.1.call-start
  8.7 1.8 reshape_squeeze.6
  10.5 2.6 reshape_squeeze.7
  13.2 0.5 fusion.6
  13.8 1.0 multiply_cosine_fusion
  14.7 79.7 %all-gather.5.cloned.1.call-done = bf16[4608,1024]{1,0:T(8,128)(2,1)} async-done(((bf16[288,1024]{1,0:T(8,128)(2,1)}), bf16[4608,1024]{1,0:T(8,128)(2,1)}) %all-gather.5.cloned.1.call-update) | async-done | bytes 9437200 | tf_op jit(solution)/shard_map/all_gather | solution.py:136
  94.5 7.1 %fusion.52 = bf16[256,1024]{1,0:T(8,128)(2,1)} fusion(bf16[4608,1024]{1,0:T(8,128)(2,1)} %all-gather.5.cloned.1.call-done, bf16[1,256,4608]{2,1,0:T(8,128)(2,1)S(1)} %copy-done, f32[4608]{0:T(1024)} %param.7, f32[256]{0:T(256)S(1)} %get-tuple-element.37), kind=kOutput, calls=%fused_computation.62 | convolution fusion | flops 2420899840 | bytes 12340224 | tf_op jit(solution)/shard_map/dot_general | solution.py:139
  101.6 3.3 collective-permute-start.1
  104.9 82.4 %all-gather.3.cloned.1.call-done = bf16[4608,1024]{1,0:T(8,128)(2,1)} async-done(((bf16[288,1024]{1,0:T(8,128)(2,1)}), bf16[4608,1024]{1,0:T(8,128)(2,1)}) %all-gather.3.cloned.1.call-update) | async-done | bytes 9437200 | tf_op jit(solution)/shard_map/all_gather | solution.py:135
  187.3 12.7 %copy.55 = bf16[1024,4608]{1,0:T(8,128)(2,1)} copy(bf16[1024,4608]{0,1:T(8,128)(2,1)} %bitcast.183) | data formatting | bytes 18874368 | tf_op jit(solution)/shard_map/dot_general | solution.py:138
  200.0 5.4 %fusion.34 = f32[256,8,128]{0,2,1:T(8,128)S(1)} fusion(bf16[8,128,4608]{2,1,0:T(8,128)(2,1)} %bitcast.184, bf16[1,256,4608]{2,1,0:T(8,128)(2,1)S(1)} %copy-done, f32[4608]{0:T(1024)} %param.7, f32[256]{0:T(256)S(1)} %get-tuple-element.37), kind=kOutput, calls=%fused_computation.45 | convolution fusion | flops 2420637696 | bytes 12864512 | tf_op jit(solution)/shard_map/dot_general | solution.py:138
  205.4 0.2 multiply_subtract_fusion.1
  205.6 0.0 copy-start.4
  205.6 2.8 collective-permute-start
  208.5 1.0 fusion.25
  209.5 1.1 copy.103
  210.7 0.7 fusion.65
  211.4 0.0 collective-permute-done.1
  211.4 1.1 copy.104
  212.5 7.3 %collective-permute-done = bf16[256,1024]{0,1:T(8,128)(2,1)S(1)} collective-permute-done((bf16[256,1024]{0,1:T(8,128)(2,1)S(1)}, bf16[256,1024]{0,1:T(8,128)(2,1)S(1)}, u32[]{:S(2)}, u32[]{:S(2)}) %collective-permute-start) | collective-permute-done | bytes 524320 | tf_op jit(solution)/shard_map/ppermute | solution.py:22
  219.8 1.0 fusion.26
  220.9 2.1 fusion.30
  223.0 3.2 fusion.17
  226.2 3.2 fusion.24
  229.5 0.0 copy-start.1
  229.5 0.8 fusion.59
  230.3 1.3 collective-permute-start.2
  231.6 1.6 fusion.60
  233.2 1.5 collective-permute-start.3
  234.8 12.8 %collective-permute-done.2 = bf16[256,8,128]{0,2,1:T(8,128)(2,1)S(1)} collective-permute-done((bf16[256,8,128]{0,2,1:T(8,128)(2,1)S(1)}, bf16[256,8,128]{0,2,1:T(8,128)(2,1)S(1)}, u32[]{:S(2)}, u32[]{:S(2)}) %collective-permute-start.2) | collective-permute-done | bytes 524320 | tf_op jit(solution)/shard_map/ppermute | solution.py:22
  247.5 0.8 convert_add_fusion
  248.4 0.2 multiply_add_fusion
  248.5 0.0 copy-start.15
  248.6 8.9 %collective-permute-done.3 = bf16[256,8,128]{0,2,1:T(8,128)(2,1)S(1)} collective-permute-done((bf16[256,8,128]{0,2,1:T(8,128)(2,1)S(1)}, bf16[256,8,128]{0,2,1:T(8,128)(2,1)S(1)}, u32[]{:S(2)}, u32[]{:S(2)}) %collective-permute-start.3) | collective-permute-done | bytes 524320 | tf_op jit(solution)/shard_map/ppermute | solution.py:22
  257.5 1.6 add_convert_fusion.1
  259.1 0.0 copy-start.11
  259.1 8.0 %fusion.36 = f32[4608,1024]{0,1:T(8,128)} fusion(bf16[256,1024]{0,1:T(8,128)(2,1)S(1)} %bitcast.191, bf16[1,256,4608]{2,1,0:T(8,128)(2,1)S(1)} %copy-done, f32[4608]{0:T(1024)S(1)} %copy-done.15, f32[256]{0:T(256)S(1)} %get-tuple-element.37), kind=kOutput, calls=%fused_computation.47 | convolution fusion | flops 2420637696 | bytes 21777408 | tf_op jit(solution)/shard_map/td,tk->dk/dot_general | solution.py:170
  267.2 0.0 copy-start.5
  267.2 0.8 copy-done.5
  268.0 8.0 %fusion.38 = f32[4608,1024]{0,1:T(8,128)} fusion(bf16[256,1024]{0,1:T(8,128)(2,1)S(1)} %bitcast.186, bf16[1,256,4608]{2,1,0:T(8,128)(2,1)S(1)} %copy-done, f32[4608]{0:T(1024)S(1)} %copy-done.15, f32[256]{0:T(256)S(1)} %get-tuple-element.37), kind=kOutput, calls=%fused_computation.49 | convolution fusion | flops 2420637696 | bytes 21777408 | tf_op jit(solution)/shard_map/td,tk->dk/dot_general | solution.py:169
  276.0 20.1 %fusion = bf16[4608,2048]{0,1:T(8,128)(2,1)} fusion(f32[4608,1024]{0,1:T(8,128)} %fusion.36, f32[4608,1024]{0,1:T(8,128)} %fusion.38), kind=kLoop, calls=%fused_computation.1 | loop fusion | flops 28311552 | bytes 56623104 | tf_op jit(solution)/shard_map/convert_element_type | solution.py:172
  296.1 24.7 %copy.101 = bf16[4608,2048]{1,0:T(8,128)(2,1)} copy(bf16[4608,2048]{0,1:T(8,128)(2,1)} %fusion) | data formatting | bytes 37748736
  320.7 0.0 reduce-scatter.4.cloned.1.call-update
  320.8 0.6 copy-done.16
  321.4 0.6 dynamic-slice
  322.7 2.2 fusion.81
  324.8 0.0 copy-done.3
  324.9 1.5 add_convert_fusion
  326.4 1.4 copy.74
  327.8 7.5 %fusion.95 = f32[256,4608]{1,0:T(8,128)S(1)} fusion(bf16[256,1024]{0,1:T(8,128)(2,1)} %bitcast.187, bf16[4608,1024]{1,0:T(8,128)(2,1)} %all-gather.3.cloned.1.call-done), kind=kOutput, calls=%fused_computation.107 | convolution fusion | flops 2415919104 | bytes 14680064 | tf_op jit(solution)/shard_map/tk,dk->td/dot_general | solution.py:179
  335.4 11.8 %fusion.14 = (f32[4608]{0:T(1024)S(1)}, f32[256]{0:T(256)S(1)}, f32[256,4608]{1,0:T(8,128)}) fusion(bf16[1,256,4608]{2,1,0:T(8,128)(2,1)S(1)} %copy-done, f32[256]{0:T(256)S(1)} %get-tuple-element.37, f32[4608]{0:T(1024)S(1)} %copy-done.15, f32[256,4608]{1,0:T(8,128)S(1)} %fusion.95, bf16[256,1024]{0,1:T(8,128)(2,1)S(1)} %bitcast.192, ...), kind=kOutput, calls=%fused_computation.18 | convolution fusion | flops 2425351424 | bytes 21796864 | tf_op jit(solution)/shard_map/tk,dk->td/dot_general | solution.py:182
  347.1 61.3 %all-reduce = f32[4608]{0:T(1024)S(1)} all-reduce(f32[4608]{0:T(1024)S(1)} %broadcast_multiply_fusion), channel_id=3, replica_groups=mesh['groups'=2,'ctx'=8,'dp'=2] {'ctx','dp'}, use_global_device_ids=true, to_apply=%region_10.11.clone | all-reduce | flops 4608 | bytes 36864
  408.5 0.7 dynamic-slice.1
  409.1 5.4 %fusion.31 = bf16[1,256,4608]{2,1,0:T(8,128)(2,1)} fusion(bf16[1,256,4608]{2,1,0:T(8,128)(2,1)S(1)} %copy-done, f32[256,4608]{1,0:T(8,128)} %get-tuple-element.43, f32[256]{0:T(256)S(1)} %broadcast_multiply_fusion.1, f32[256]{0:T(256)S(1)} %get-tuple-element.36, f32[4608]{0:T(1024)S(1)} %copy-done.15, f32[256]{0:T(256)S(1)} %get-tuple-element.37), kind=kLoop, calls=%fused_computation.43 | loop fusion | flops 8257536 | bytes 9458688 | tf_op jit(solution)/shard_map/broadcast_in_dim | solution.py:192
  414.5 101.2 %reduce-scatter.4.cloned.1.call-done = bf16[288,2048]{1,0:T(8,128)(2,1)} async-done(((bf16[4608,2048]{1,0:T(8,128)(2,1)}), bf16[288,2048]{1,0:T(8,128)(2,1)}) %reduce-scatter.4.cloned.1.call-update) | async-done | bytes 1179664
  515.7 1.8 copy.102
  517.5 1.8 fusion.94
  519.4 2.9 copy.76
  522.2 2.9 copy.75
  (37 shorter events, 0.3 us)
Async XLA Ops:
  7.2 6.0 %copy-start = (bf16[1,256,4608]{2,1,0:T(8,128)(2,1)S(1)}, bf16[1,256,4608]{2,1,0:T(8,128)(2,1)}, u32[]{:S(2)}) copy-start(bf16[1,256,4608]{2,1,0:T(8,128)(2,1)} %param.6) | copy-start | bytes 7077892
  7.2 87.3 %all-gather.5.cloned.1.call-start = ((), (), s32[]{:S(2)}) async-start(), calls=%async_computation.2 | async-start | bytes 10027008 | tf_op jit(solution)/shard_map/all_gather | solution.py:136
  7.9 179.3 %all-gather.3.cloned.1.call-start = ((), (), s32[]{:S(2)}) async-start(), calls=%async_computation.1 | async-start | bytes 10027008 | tf_op jit(solution)/shard_map/all_gather | solution.py:135
  8.7 507.1 %reduce-scatter.4.cloned.1.call-start = ((), (), s32[]{:S(2)}) async-start(), calls=%async_computation.3 | async-start | bytes 20054016
  101.6 109.8 %collective-permute-start.1 = (bf16[256,1024]{1,0:T(8,128)(2,1)}, bf16[256,1024]{1,0:T(8,128)(2,1)}, u32[]{:S(2)}, u32[]{:S(2)}) collective-permute-start(bf16[256,1024]{1,0:T(8,128)(2,1)} %fusion.52), channel_id=1, source_target_pairs={{0,2},{2,4},{4,6},{6,8},{8,10},{10,12},{12,14},{1,3},{3,5},{5,7},{... | collective-permute-start | bytes 1572872 | tf_op jit(solution)/shard_map/ppermute | solution.py:22
  200.0 5.4 %copy-start.13 = (f32[256,64]{0,1:T(8,128)S(1)}, f32[256,64]{0,1:T(8,128)}, u32[]{:S(2)}) copy-start(f32[256,64]{0,1:T(8,128)} %get-tuple-element.34) | copy-start | bytes 196612
  200.0 5.4 %copy-start.14 = (f32[256,64]{0,1:T(8,128)S(1)}, f32[256,64]{0,1:T(8,128)}, u32[]{:S(2)}) copy-start(f32[256,64]{0,1:T(8,128)} %get-tuple-element.35) | copy-start | bytes 196612
  205.6 5.1 copy-start.6
  205.6 5.1 copy-start.8
  205.6 5.1 copy-start.4
  205.6 14.2 %collective-permute-start = (bf16[256,1024]{0,1:T(8,128)(2,1)S(1)}, bf16[256,1024]{0,1:T(8,128)(2,1)S(1)}, u32[]{:S(2)}, u32[]{:S(2)}) collective-permute-start(bf16[256,1024]{0,1:T(8,128)(2,1)S(1)} %bitcast.194), channel_id=1, source_target_pairs={{0,2},{2,4},{4,6},{6,8},{8,10},{10,12},{12,14},{1,3},{3,5},{5,7},{... | collective-permute-start | bytes 1572872 | tf_op jit(solution)/shard_map/ppermute | solution.py:22
  219.8 3.1 copy-start.10
  229.5 3.8 copy-start.2
  229.5 18.0 %copy-start.1 = (bf16[8,2,256,256]{2,3,1,0:T(8,128)(2,1)}, bf16[8,2,256,256]{2,3,1,0:T(8,128)(2,1)S(1)}, u32[]{:S(2)}) copy-start(bf16[8,2,256,256]{2,3,1,0:T(8,128)(2,1)S(1)} %get-tuple-element.32) | copy-start | bytes 6291460
  230.3 17.2 %collective-permute-start.2 = (bf16[256,8,128]{0,2,1:T(8,128)(2,1)S(1)}, bf16[256,8,128]{0,2,1:T(8,128)(2,1)S(1)}, u32[]{:S(2)}, u32[]{:S(2)}) collective-permute-start(bf16[256,8,128]{0,2,1:T(8,128)(2,1)S(1)} %fusion.59), channel_id=1, source_target_pairs={{2,0},{4,2},{6,4},{8,6},{10,8},{12,10},{14,12},{3,1},{5,3},{7,5},{... | collective-permute-start | bytes 1572872 | tf_op jit(solution)/shard_map/ppermute | solution.py:22
  233.2 24.2 %collective-permute-start.3 = (bf16[256,8,128]{0,2,1:T(8,128)(2,1)S(1)}, bf16[256,8,128]{0,2,1:T(8,128)(2,1)S(1)}, u32[]{:S(2)}, u32[]{:S(2)}) collective-permute-start(bf16[256,8,128]{0,2,1:T(8,128)(2,1)S(1)} %fusion.60), channel_id=1, source_target_pairs={{2,0},{4,2},{6,4},{8,6},{10,8},{12,10},{14,12},{3,1},{5,3},{7,5},{... | collective-permute-start | bytes 1572872 | tf_op jit(solution)/shard_map/ppermute | solution.py:22
  248.5 10.6 %copy-start.15 = (f32[4608]{0:T(1024)S(1)}, f32[4608]{0:T(1024)}, u32[]{:S(2)}) copy-start(f32[4608]{0:T(1024)} %param.7) | copy-start | bytes 55300
  259.1 8.0 %copy-start.11 = (bf16[256,8,128]{0,2,1:T(8,128)(2,1)}, bf16[256,8,128]{0,2,1:T(8,128)(2,1)S(1)}, u32[]{:S(2)}) copy-start(bf16[256,8,128]{0,2,1:T(8,128)(2,1)S(1)} %add_convert_fusion.1) | copy-start | bytes 1572868
  267.2 0.8 copy-start.5
  320.7 0.7 copy-start.16
  320.7 1.9 copy-start.7
  320.7 1.9 copy-start.9
  322.6 2.2 copy-start.3
  327.8 7.5 %copy-start.12 = (bf16[256,8,128]{0,2,1:T(8,128)(2,1)S(1)}, bf16[256,8,128]{0,2,1:T(8,128)(2,1)}, u32[]{:S(2)}) copy-start(bf16[256,8,128]{0,2,1:T(8,128)(2,1)} %copy-done.11) | copy-start | bytes 1572868
Sparse Core Ops, SparseCore 0:
  10.3 84.1 all-gather.4
  96.8 90.4 all-gather.2
  320.9 194.7 reduce-scatter.3
where the time goes:
time: 533 us; the launch traced here: 532 us
  waiting for transfers between devices  294 us (55%)
  matrix products  62.4 us (12%)
  blocking collectives  61.3 us (12%)
  local copies, waits for them, and re-layouts  57.5 us (11%)
  other arithmetic  32.8 us (6%)
  between operations  14.8 us (3%)
  starting transfers between devices  8.97 us (2%)
    unnamed x4, waiting for transfers between devices  103 us
    all_gather x1, waiting for transfers between devices, body(): lax.all_gather(key_weight, ('ctx', 'dp'), axis=0, tiled=True)  82.4 us
    all_gather x1, waiting for transfers between devices, body(): lax.all_gather(value_weight, ('ctx', 'dp'), axis=0, tiled=True)  79.7 us
    unnamed x1, blocking collectives  61.3 us
    unnamed x43, local copies, waits for them, and re-layouts  38.6 us
    ppermute x4, waiting for transfers between devices, from_behind(): lax.ppermute(value, axis, [(source, source + steps) for source in range(i...  29 us
    convert_element_type x1, other arithmetic, body(): (jnp.concatenate([key_part, value_part], axis=1) * grad_scale).astype(jnp...  20.1 us
    dot_general x1, local copies, waits for them, and re-layouts, body(): key_raw = jnp.dot(normed, full_key, preferred_element_type=jnp.float32)  12.7 us
  transfers between devices with their start and end apart: 7, of which 6 were waited for; matrix products, arithmetic and copies ran while one was open for 13% of the time, Pallas kernels for 0%

commit v1 on v0

--- a/solution.py
+++ b/solution.py
@@ -131,12 +131,29 @@
     inputs = hidden_in[0].astype(jnp.float32)
     inverse = lax.rsqrt(jnp.mean(inputs * inputs, axis=-1, keepdims=True) + norm_eps)
     normed = (inputs * inverse * norm_gain).astype(jnp.bfloat16)
-    full_key, full_value = (
-        lax.all_gather(key_weight, ("ctx", "dp"), axis=0, tiled=True),
-        lax.all_gather(value_weight, ("ctx", "dp"), axis=0, tiled=True),
-    )
-    key_raw = jnp.dot(normed, full_key, preferred_element_type=jnp.float32)
-    value_rows = jnp.dot(normed, full_value, preferred_element_type=jnp.float32).astype(
+    n_ctx = lax.axis_size("ctx")
+    n_dp = lax.axis_size("dp")
+    model_width = normed.shape[1]
+    shard_rows = model_width // (n_ctx * n_dp)
+
+    def to_dp_major(rows):
+        lead = rows.shape[:-1]
+        split = rows.reshape(lead + (n_ctx, n_dp, shard_rows))
+        return jnp.swapaxes(split, -3, -2).reshape(lead + (model_width,))
+
+    def from_dp_major(rows):
+        lead = rows.shape[:-1]
+        split = rows.reshape(lead + (n_dp, n_ctx, shard_rows))
+        return jnp.swapaxes(split, -3, -2).reshape(lead + (model_width,))
+
+    def gather_rows(weight):
+        by_ctx = lax.all_gather(weight, "ctx", axis=0, tiled=True)
+        return lax.all_gather(by_ctx, "dp", axis=0, tiled=True)
+
+    full_key, full_value = gather_rows(key_weight), gather_rows(value_weight)
+    normed_perm = to_dp_major(normed)
+    key_raw = jnp.dot(normed_perm, full_key, preferred_element_type=jnp.float32)
+    value_rows = jnp.dot(normed_perm, full_value, preferred_element_type=jnp.float32).astype(
         jnp.bfloat16
     )
     ctx_index = lax.axis_index("ctx")
@@ -166,14 +183,15 @@
         .reshape(tok_rows, key_width)
     )
     value_low = value_grad.astype(jnp.bfloat16).reshape(tok_rows, key_width)
-    key_part = jnp.einsum("td,tk->dk", normed, key_grad_raw, preferred_element_type=jnp.float32)
-    value_part = jnp.einsum("td,tk->dk", normed, value_low, preferred_element_type=jnp.float32)
-    stacked = lax.psum_scatter(
-        (jnp.concatenate([key_part, value_part], axis=1) * grad_scale).astype(jnp.bfloat16),
-        ("ctx", "dp"),
-        scatter_dimension=0,
-        tiled=True,
-    ).astype(jnp.float32)
+    key_part = jnp.einsum(
+        "td,tk->dk", normed_perm, key_grad_raw, preferred_element_type=jnp.float32
+    )
+    value_part = jnp.einsum(
+        "td,tk->dk", normed_perm, value_low, preferred_element_type=jnp.float32
+    )
+    terms = (jnp.concatenate([key_part, value_part], axis=1) * grad_scale).astype(jnp.bfloat16)
+    terms = lax.psum_scatter(terms, "dp", scatter_dimension=0, tiled=True)
+    stacked = lax.psum_scatter(terms, "ctx", scatter_dimension=0, tiled=True).astype(jnp.float32)
     key_weight_grad = stacked[:, :key_width]
     value_weight_grad = stacked[:, key_width:]
     normed_grad = jnp.einsum(
@@ -182,13 +200,15 @@
     normed_grad = normed_grad + jnp.einsum(
         "tk,dk->td", value_low, full_value, preferred_element_type=jnp.float32
     )
+    normed_grad = from_dp_major(normed_grad)
     scaled = normed_grad * norm_gain
     cubed = inverse * inverse * inverse
     hidden_grad = (
         inverse * scaled - inputs * cubed * jnp.mean(scaled * inputs, axis=-1, keepdims=True)
     ).astype(jnp.bfloat16)
     gain_term = jnp.sum(normed_grad * inputs * inverse, axis=0) * grad_scale
-    gain_grad = lax.psum_scatter(gain_term, ("ctx", "dp"), scatter_dimension=0, tiled=True)
+    gain_term = lax.psum_scatter(to_dp_major(gain_term), "dp", scatter_dimension=0, tiled=True)
+    gain_grad = lax.psum_scatter(gain_term, "ctx", scatter_dimension=0, tiled=True)
     return (hidden_grad[None], query_gradient[None], key_weight_grad, value_weight_grad, gain_grad)
 
 

time: 533 us -> 551 us (1.034)
  waiting for transfers between devices: 294 us -> 327 us
  blocking collectives: 61.3 us -> 43.3 us
  matrix products: 62.4 us -> 50.5 us
  local copies, waits for them, and re-layouts: 57.5 us -> 63.3 us
  other arithmetic: 32.8 us -> 38.4 us
    reduce_scatter x0 -> x1, waiting for transfers between devices: none -> 29.6 us  [body(): terms = lax.psum_scatter(terms, 'dp', scatter_dimension=0, tiled=True)]
    all_gather x2 -> x4, waiting for transfers between devices: 162 us -> 188 us  [the longest x2 164 us: gather_rows(): by_ctx = lax.all_gather(weight, 'ctx', axis=0, tiled=True)]
    unnamed x4 -> x7, waiting for transfers between devices: 103 us -> 80.2 us
    unnamed x1 -> x2, blocking collectives: 61.3 us -> 43.3 us
    dot_general x1, matrix products: 11.8 us -> 4.42 us  [body(): jnp.einsum('tk,dk->td', value_low, full_value, preferred_element_type=jnp...]
    add x0 -> x1, local copies, waits for them, and re-layouts: none -> 6.08 us  [body(): normed_grad + jnp.einsum('tk,dk->td', value_low, full_value, preferred_el...]
    unnamed x43 -> x75, local copies, waits for them, and re-layouts: 38.6 us -> 35.3 us
  transfers between devices with their start and end apart: 7 -> 10, of which waited for: 6 -> 9; matrix products, arithmetic and copies ran while one was open for 13% -> 15% of each run, Pallas kernels for 0% -> 0%
where the time goes in v1:
time: 551 us; the launch traced here: 550 us
  waiting for transfers between devices  327 us (59%)
  local copies, waits for them, and re-layouts  63.3 us (11%)
  matrix products  50.5 us (9%)
  blocking collectives  43.3 us (8%)
  other arithmetic  38.4 us (7%)
  between operations  15.9 us (3%)
  starting transfers between devices  11.4 us (2%)
    all_gather x2, waiting for transfers between devices, gather_rows(): by_ctx = lax.all_gather(weight, 'ctx', axis=0, tiled=True)  164 us
    unnamed x7, waiting for transfers between devices  80.2 us
    unnamed x2, blocking collectives  43.3 us
    unnamed x75, local copies, waits for them, and re-layouts  35.3 us
    reduce_scatter x1, waiting for transfers between devices, body(): terms = lax.psum_scatter(terms, 'dp', scatter_dimension=0, tiled=True)  29.6 us
    ppermute x4, waiting for transfers between devices, from_behind(): lax.ppermute(value, axis, [(source, source + steps) for source in range(i...  29.1 us
    all_gather x2, waiting for transfers between devices, gather_rows(): return lax.all_gather(by_ctx, 'dp', axis=0, tiled=True)  24.2 us
    convert_element_type x1, other arithmetic, body(): (jnp.concatenate([key_part, value_part], axis=1) * grad_scale).astype(jnp...  20 us
  transfers between devices with their start and end apart: 10, of which 9 were waited for; matrix products, arithmetic and copies ran while one was open for 15% of the time, Pallas kernels for 0%

profile of v1, /device:TPU:0, one launch (start us, length us, event | category | flops | bytes accessed | tf_op | source)
XLA Modules:
  0.0 550.2 jit_solution(13586467469445376264)
XLA Ops:
  7.2 0.7 all-gather.9.cloned.1.call-update
  7.9 0.7 all-gather.5.cloned.1.call-update
  8.7 84.1 %all-gather.9.cloned.1.call-done = bf16[2304,1024]{1,0:T(8,128)(2,1)} async-done(((bf16[288,1024]{1,0:T(8,128)(2,1)}), bf16[2304,1024]{1,0:T(8,128)(2,1)}) %all-gather.9.cloned.1.call-update) | async-done | bytes 4718608 | tf_op jit(solution)/shard_map/all_gather | solution.py:150
  92.9 80.2 %all-gather.5.cloned.1.call-done = bf16[2304,1024]{1,0:T(8,128)(2,1)} async-done(((bf16[288,1024]{1,0:T(8,128)(2,1)}), bf16[2304,1024]{1,0:T(8,128)(2,1)}) %all-gather.5.cloned.1.call-update) | async-done | bytes 4718608 | tf_op jit(solution)/shard_map/all_gather | solution.py:150
  173.2 0.8 reshape_squeeze.6
  174.0 1.5 reshape_squeeze.7
  175.6 2.8 copy.65
  178.4 0.6 multiply_reduce_fusion
  179.1 2.8 fusion.19
  181.9 0.2 copy-done.1
  182.4 1.0 multiply_cosine_fusion
  183.3 11.3 %all-gather.11.cloned.1.call-done = bf16[4608,1024]{1,0:T(8,128)(2,1)} async-done(((bf16[2304,1024]{1,0:T(8,128)(2,1)}), bf16[4608,1024]{1,0:T(8,128)(2,1)}) %all-gather.11.cloned.1.call-update) | async-done | bytes 9437200 | tf_op jit(solution)/shard_map/all_gather | solution.py:151
  194.6 7.1 %convolution_convert_fusion = bf16[256,1024]{1,0:T(8,128)(2,1)} fusion(bf16[256,4608]{0,1:T(8,128)(2,1)S(1)} %bitcast.166, bf16[4608,1024]{1,0:T(8,128)(2,1)} %all-gather.11.cloned.1.call-done), kind=kOutput, calls=%fused_computation.44 | convolution fusion | flops 2416181248 | bytes 12320768 | tf_op jit(solution)/shard_map/dot_general | solution.py:156
  201.7 4.4 collective-permute-start.1
  206.1 12.9 %all-gather.7.cloned.1.call-done = bf16[4608,1024]{1,0:T(8,128)(2,1)} async-done(((bf16[2304,1024]{1,0:T(8,128)(2,1)}), bf16[4608,1024]{1,0:T(8,128)(2,1)}) %all-gather.7.cloned.1.call-update) | async-done | bytes 9437200 | tf_op jit(solution)/shard_map/all_gather | solution.py:151
  219.1 12.7 %copy.67 = bf16[1024,4608]{1,0:T(8,128)(2,1)} copy(bf16[1024,4608]{0,1:T(8,128)(2,1)} %bitcast.176) | data formatting | bytes 18874368 | tf_op jit(solution)/shard_map/dot_general | solution.py:155
  231.8 5.2 fusion.67
  237.2 4.0 collective-permute-start
  241.2 1.0 fusion.13
  242.3 1.1 copy.122
  243.4 0.7 fusion.40
  244.2 1.1 copy.123
  245.3 7.3 %collective-permute-done = bf16[256,1024]{0,1:T(8,128)(2,1)S(1)} collective-permute-done((bf16[256,1024]{0,1:T(8,128)(2,1)S(1)}, bf16[256,1024]{0,1:T(8,128)(2,1)S(1)}, u32[]{:S(2)}, u32[]{:S(2)}) %collective-permute-start) | collective-permute-done | bytes 524320 | tf_op jit(solution)/shard_map/ppermute | solution.py:22
  252.7 1.0 fusion.14
  253.7 2.1 fusion.18
  255.8 3.2 fusion.5
  259.1 3.2 fusion.12
  262.3 0.8 fusion.34
  263.1 1.3 collective-permute-start.2
  264.4 1.6 fusion.35
  266.1 1.5 collective-permute-start.3
  267.6 12.7 %collective-permute-done.2 = bf16[256,8,128]{0,2,1:T(8,128)(2,1)S(1)} collective-permute-done((bf16[256,8,128]{0,2,1:T(8,128)(2,1)S(1)}, bf16[256,8,128]{0,2,1:T(8,128)(2,1)S(1)}, u32[]{:S(2)}, u32[]{:S(2)}) %collective-permute-start.2) | collective-permute-done | bytes 524320 | tf_op jit(solution)/shard_map/ppermute | solution.py:22
  280.3 0.8 convert_add_fusion
  281.3 9.0 %collective-permute-done.3 = bf16[256,8,128]{0,2,1:T(8,128)(2,1)S(1)} collective-permute-done((bf16[256,8,128]{0,2,1:T(8,128)(2,1)S(1)}, bf16[256,8,128]{0,2,1:T(8,128)(2,1)S(1)}, u32[]{:S(2)}, u32[]{:S(2)}) %collective-permute-start.3) | collective-permute-done | bytes 524320 | tf_op jit(solution)/shard_map/ppermute | solution.py:22
  290.3 1.6 add_convert_fusion.1
  292.0 7.9 %fusion.70 = f32[4608,1024]{0,1:T(8,128)} fusion(bf16[256,4608]{0,1:T(8,128)(2,1)S(1)} %bitcast.168, bf16[256,1024]{0,1:T(8,128)(2,1)S(1)} %bitcast.186), kind=kOutput, calls=%fused_computation.92 | convolution fusion | flops 2415919104 | bytes 21757952 | tf_op jit(solution)/shard_map/td,tk->dk/dot_general | solution.py:189
  299.9 0.8 copy-done.14
  300.7 7.9 %fusion.69 = f32[4608,1024]{0,1:T(8,128)} fusion(bf16[256,4608]{0,1:T(8,128)(2,1)S(1)} %bitcast.169, bf16[256,1024]{0,1:T(8,128)(2,1)S(1)} %bitcast.182), kind=kOutput, calls=%fused_computation.91 | convolution fusion | flops 2415919104 | bytes 21757952 | tf_op jit(solution)/shard_map/td,tk->dk/dot_general | solution.py:186
  308.6 20.0 %fusion = bf16[4608,2048]{0,1:T(8,128)(2,1)} fusion(f32[4608,1024]{0,1:T(8,128)} %fusion.70, f32[4608,1024]{0,1:T(8,128)} %fusion.69), kind=kLoop, calls=%fused_computation.1 | loop fusion | flops 28311552 | bytes 56623104 | tf_op jit(solution)/shard_map/convert_element_type | solution.py:192
  328.7 29.6 %reduce-scatter.5.cloned.1.call-done = bf16[2304,2048]{0,1:T(8,128)(2,1)} async-done(((bf16[4608,2048]{0,1:T(8,128)(2,1)}), bf16[2304,2048]{0,1:T(8,128)(2,1)}) %reduce-scatter.5.cloned.1.call-update) | async-done | bytes 9437200 | tf_op jit(solution)/shard_map/reduce_scatter | solution.py:193
  358.3 12.7 %copy.120 = bf16[2304,2048]{1,0:T(8,128)(2,1)} copy(bf16[2304,2048]{0,1:T(8,128)(2,1)} %reduce-scatter.5.cloned.1.call-done) | data formatting | bytes 18874368
  371.1 0.6 copy-done.27
  371.7 0.6 dynamic-slice.2
  372.3 0.6 dynamic-slice
  374.2 0.4 fusion.56
  374.7 1.1 copy-done.6
  375.8 0.5 add_convert_fusion
  376.3 1.4 copy.91
  377.8 6.2 %fusion.68 = f32[256,4608]{1,0:T(8,128)S(1)} fusion(bf16[256,1024]{0,1:T(8,128)(2,1)S(1)} %bitcast.183, bf16[4608,1024]{1,0:T(8,128)(2,1)} %all-gather.7.cloned.1.call-done), kind=kOutput, calls=%fused_computation.90 | convolution fusion | flops 2415919104 | bytes 14680064 | tf_op jit(solution)/shard_map/tk,dk->td/dot_general | solution.py:197
  384.0 0.8 slice-done.2
  384.8 4.4 convolution_add_fusion
  389.3 6.1 %copy.85 = f32[256,4608]{0,1:T(8,128)} copy(f32[256,4608]{1,0:T(8,128)} %convolution_add_fusion) | data formatting | bytes 9437184 | tf_op jit(solution)/shard_map/add | solution.py:200
  395.3 5.2 copy.86
  400.5 3.5 fusion.2
  404.2 4.6 subtract_convert_fusion
  408.8 4.3 copy.90
  413.1 3.5 all-reduce
  416.7 39.8 %all-reduce.1 = f32[2304]{0:T(1024)S(1)} all-reduce(f32[2304]{0:T(1024)S(1)} %dynamic-slice.1), channel_id=5, replica_groups=mesh['groups'=2,'ctx'=8,'dp'=2] {'ctx'}, use_global_device_ids=true, to_apply=%region_12.13.clone | all-reduce | flops 2304 | bytes 18432
  456.4 0.7 dynamic-slice.3
  457.1 78.7 %reduce-scatter.7.cloned.1.call-done = bf16[288,2048]{1,0:T(8,128)(2,1)} async-done(((bf16[2304,2048]{1,0:T(8,128)(2,1)}), bf16[288,2048]{1,0:T(8,128)(2,1)}) %reduce-scatter.7.cloned.1.call-update) | async-done | bytes 1179664
  535.8 1.8 copy.121
  537.6 1.4 fusion.66
  539.0 2.9 copy.93
  541.9 1.5 copy.92
  (88 shorter events, 1.4 us)
Async XLA Ops:
  7.2 85.6 %all-gather.9.cloned.1.call-start = ((), (), s32[]{:S(2)}) async-start(), calls=%async_computation.4 | async-start | bytes 5308416 | tf_op jit(solution)/shard_map/all_gather | solution.py:150
  7.9 165.1 %all-gather.5.cloned.1.call-start = ((), (), s32[]{:S(2)}) async-start(), calls=%async_computation.2 | async-start | bytes 5308416 | tf_op jit(solution)/shard_map/all_gather | solution.py:150
  8.6 186.0 %all-gather.11.cloned.1.call-start = ((), (), s32[]{:S(2)}) async-start(), calls=%async_computation.5 | async-start | bytes 14155776 | tf_op jit(solution)/shard_map/all_gather | solution.py:151
  92.8 80.3 %copy-start.24 = (f32[4608]{0:T(1024)S(1)}, f32[4608]{0:T(1024)}, u32[]{:S(2)}) copy-start(f32[4608]{0:T(1024)} %param.7) | copy-start | bytes 55300
  92.8 80.4 %copy-start.16 = (bf16[1,256,2048]{2,1,0:T(8,128)(2,1)S(1)}, bf16[1,256,2048]{2,1,0:T(8,128)(2,1)}, u32[]{:S(2)}) copy-start(bf16[1,256,2048]{2,1,0:T(8,128)(2,1)} %param.10) | copy-start | bytes 3145732
  92.8 81.2 %copy-start.17 = (bf16[1,256,2048]{2,1,0:T(8,128)(2,1)S(1)}, bf16[1,256,2048]{2,1,0:T(8,128)(2,1)}, u32[]{:S(2)}) copy-start(bf16[1,256,2048]{2,1,0:T(8,128)(2,1)} %param.11) | copy-start | bytes 3145732
  92.8 126.2 %all-gather.7.cloned.1.call-start = ((), (), s32[]{:S(2)}) async-start(), calls=%async_computation.3 | async-start | bytes 14155776 | tf_op jit(solution)/shard_map/all_gather | solution.py:151
  173.1 185.2 %reduce-scatter.5.cloned.1.call-start = ((), (), s32[]{:S(2)}) async-start(), calls=%async_computation.6 | async-start | bytes 28311552 | tf_op jit(solution)/shard_map/reduce_scatter | solution.py:193
  173.2 5.8 %copy-start.22 = (f32[8,2,288]{2,1,0:T(2,128)}, f32[8,2,288]{2,1,0:T(2,128)S(1)}, u32[]{:S(2)}) copy-start(f32[8,2,288]{2,1,0:T(2,128)S(1)} %mul.232) | copy-start | bytes 55300
  178.4 3.7 copy-start.1
  201.7 42.4 %collective-permute-start.1 = (bf16[256,1024]{1,0:T(8,128)(2,1)}, bf16[256,1024]{1,0:T(8,128)(2,1)}, u32[]{:S(2)}, u32[]{:S(2)}) collective-permute-start(bf16[256,1024]{1,0:T(8,128)(2,1)} %convolution_convert_fusion), channel_id=1, source_target_pairs={{0,2},{2,4},{4,6},{6,8},{8,10},{10,12},{12,14},{1,3},{3,5},{5,7},{... | collective-permute-start | bytes 1572872 | tf_op jit(solution)/shard_map/ppermute | solution.py:22
  231.7 5.2 copy-start.18
  231.8 5.2 copy-start.19
  237.2 6.2 %copy-start.8 = (bf16[256,8,64]{0,2,1:T(8,128)(2,1)}, bf16[256,8,64]{0,2,1:T(8,128)(2,1)S(1)}, u32[]{:S(2)}) copy-start(bf16[256,8,64]{0,2,1:T(8,128)(2,1)S(1)} %get-tuple-element.32) | copy-start | bytes 786436
  237.2 6.2 %copy-start.10 = (bf16[256,8,64]{0,2,1:T(8,128)(2,1)}, bf16[256,8,64]{0,2,1:T(8,128)(2,1)S(1)}, u32[]{:S(2)}) copy-start(bf16[256,8,64]{0,2,1:T(8,128)(2,1)S(1)} %get-tuple-element.33) | copy-start | bytes 786436
  237.2 6.2 %copy-start.7 = (bf16[256,8,2,128]{3,2,1,0:T(2,128)(2,1)S(1)}, bf16[256,8,2,128]{3,2,1,0:T(2,128)(2,1)}, u32[]{:S(2)}) copy-start(bf16[256,8,2,128]{3,2,1,0:T(2,128)(2,1)} %reshape_squeeze.7) | copy-start | bytes 3145732
  237.2 15.4 %collective-permute-start = (bf16[256,1024]{0,1:T(8,128)(2,1)S(1)}, bf16[256,1024]{0,1:T(8,128)(2,1)S(1)}, u32[]{:S(2)}, u32[]{:S(2)}) collective-permute-start(bf16[256,1024]{0,1:T(8,128)(2,1)S(1)} %bitcast.185), channel_id=1, source_target_pairs={{0,2},{2,4},{4,6},{6,8},{8,10},{10,12},{12,14},{1,3},{3,5},{5,7},{... | collective-permute-start | bytes 1572872 | tf_op jit(solution)/shard_map/ppermute | solution.py:22
  252.6 3.1 copy-start.12
  262.3 3.8 copy-start.5
  262.3 18.0 %copy-start.3 = (bf16[8,2,256,256]{2,3,1,0:T(8,128)(2,1)}, bf16[8,2,256,256]{2,3,1,0:T(8,128)(2,1)S(1)}, u32[]{:S(2)}) copy-start(bf16[8,2,256,256]{2,3,1,0:T(8,128)(2,1)S(1)} %get-tuple-element.34) | copy-start | bytes 6291460
  263.1 17.2 %collective-permute-start.2 = (bf16[256,8,128]{0,2,1:T(8,128)(2,1)S(1)}, bf16[256,8,128]{0,2,1:T(8,128)(2,1)S(1)}, u32[]{:S(2)}, u32[]{:S(2)}) collective-permute-start(bf16[256,8,128]{0,2,1:T(8,128)(2,1)S(1)} %fusion.34), channel_id=1, source_target_pairs={{2,0},{4,2},{6,4},{8,6},{10,8},{12,10},{14,12},{3,1},{5,3},{7,5},{... | collective-permute-start | bytes 1572872 | tf_op jit(solution)/shard_map/ppermute | solution.py:22
  266.1 24.3 %collective-permute-start.3 = (bf16[256,8,128]{0,2,1:T(8,128)(2,1)S(1)}, bf16[256,8,128]{0,2,1:T(8,128)(2,1)S(1)}, u32[]{:S(2)}, u32[]{:S(2)}) collective-permute-start(bf16[256,8,128]{0,2,1:T(8,128)(2,1)S(1)} %fusion.35), channel_id=1, source_target_pairs={{2,0},{4,2},{6,4},{8,6},{10,8},{12,10},{14,12},{3,1},{5,3},{7,5},{... | collective-permute-start | bytes 1572872 | tf_op jit(solution)/shard_map/ppermute | solution.py:22
  292.0 7.9 %copy-start.20 = (bf16[256,8,128]{0,2,1:T(8,128)(2,1)}, bf16[256,8,128]{0,2,1:T(8,128)(2,1)S(1)}, u32[]{:S(2)}) copy-start(bf16[256,8,128]{0,2,1:T(8,128)(2,1)S(1)} %add_convert_fusion.1) | copy-start | bytes 1572868
  299.9 0.8 copy-start.14
  328.6 207.2 %reduce-scatter.7.cloned.1.call-start = ((), (), s32[]{:S(2)}) async-start(), calls=%async_computation.7 | async-start | bytes 10616832
  371.0 0.7 copy-start.27
  371.0 1.3 copy-start.26
  371.0 3.2 copy-start.4
  371.1 3.2 copy-start.9
  371.1 3.2 copy-start.11
  371.1 3.6 copy-start.13
  374.2 1.6 copy-start.6
  375.8 1.9 copy-start.15
  375.8 8.1 %slice-start = ((s8[9437184]{0:T(1024)(128)(4,1)}), s8[1048576]{0:T(1024)(128)(4,1)S(1)}, s32[]{:S(2)}) async-start(s8[9437184]{0:T(1024)(128)(4,1)} %bitcast.173), calls=%async_computation.8 | async-start | bytes 2097152
  377.7 6.2 %slice-start.1 = ((s8[9437184]{0:T(1024)(128)(4,1)}), s8[4194304]{0:T(1024)(128)(4,1)S(1)}, s32[]{:S(2)}) async-start(s8[9437184]{0:T(1024)(128)(4,1)} %bitcast.173), calls=%async_computation.9 | async-start | bytes 8388608
  377.7 7.1 %slice-start.2 = ((s8[9437184]{0:T(1024)(128)(4,1)}), s8[4194304]{0:T(1024)(128)(4,1)S(1)}, s32[]{:S(2)}) async-start(s8[9437184]{0:T(1024)(128)(4,1)} %bitcast.173), calls=%async_computation.10 | async-start | bytes 8388608
  377.7 7.1 %copy-start.21 = (bf16[256,8,128]{0,2,1:T(8,128)(2,1)S(1)}, bf16[256,8,128]{0,2,1:T(8,128)(2,1)}, u32[]{:S(2)}) copy-start(bf16[256,8,128]{0,2,1:T(8,128)(2,1)} %copy-done.20) | copy-start | bytes 1572868
  395.3 5.2 copy-start
  395.3 5.2 copy-start.23
  400.5 3.7 copy-start.2
  400.5 3.7 copy-start.25
Sparse Core Ops, SparseCore 0:
  10.2 82.5 all-gather.8
  95.0 78.0 all-gather.4
  174.6 19.9 all-gather.10
  196.0 23.0 all-gather.6
  328.8 29.4 reduce-scatter.4
  371.2 164.5 reduce-scatter.6

commit v2 on v0

--- a/solution.py
+++ b/solution.py
@@ -131,10 +131,14 @@
     inputs = hidden_in[0].astype(jnp.float32)
     inverse = lax.rsqrt(jnp.mean(inputs * inputs, axis=-1, keepdims=True) + norm_eps)
     normed = (inputs * inverse * norm_gain).astype(jnp.bfloat16)
-    full_key, full_value = (
-        lax.all_gather(key_weight, ("ctx", "dp"), axis=0, tiled=True),
-        lax.all_gather(value_weight, ("ctx", "dp"), axis=0, tiled=True),
-    )
+    n_groups = lax.axis_size("groups")
+    group_index = lax.axis_index("groups")
+
+    def gather_rows(weight):
+        pieces = weight.reshape(n_groups, weight.shape[0] // n_groups, weight.shape[1])
+        return lax.all_gather(pieces[group_index], ("ctx", "dp", "groups"), axis=0, tiled=True)
+
+    full_key, full_value = gather_rows(key_weight), gather_rows(value_weight)
     key_raw = jnp.dot(normed, full_key, preferred_element_type=jnp.float32)
     value_rows = jnp.dot(normed, full_value, preferred_element_type=jnp.float32).astype(
         jnp.bfloat16
@@ -166,14 +170,17 @@
         .reshape(tok_rows, key_width)
     )
     value_low = value_grad.astype(jnp.bfloat16).reshape(tok_rows, key_width)
-    key_part = jnp.einsum("td,tk->dk", normed, key_grad_raw, preferred_element_type=jnp.float32)
-    value_part = jnp.einsum("td,tk->dk", normed, value_low, preferred_element_type=jnp.float32)
-    stacked = lax.psum_scatter(
-        (jnp.concatenate([key_part, value_part], axis=1) * grad_scale).astype(jnp.bfloat16),
-        ("ctx", "dp"),
-        scatter_dimension=0,
-        tiled=True,
-    ).astype(jnp.float32)
+    n_blocks = lax.axis_size("ctx") * lax.axis_size("dp")
+    shard_rows = normed.shape[1] // n_blocks
+    normed_cols = jnp.swapaxes(normed.reshape(tok_rows, n_blocks, shard_rows), 0, 1)
+    normed_cols = lax.all_to_all(normed_cols, ("ctx", "dp"), 0, 0, tiled=True)
+    grads_low = lax.all_gather(
+        jnp.concatenate([key_grad_raw, value_low], axis=1), ("ctx", "dp"), axis=0
+    )
+    block_terms = jnp.einsum(
+        "btd,btk->bdk", normed_cols, grads_low, preferred_element_type=jnp.float32
+    )
+    stacked = (block_terms * grad_scale).astype(jnp.bfloat16).astype(jnp.float32).sum(0)
     key_weight_grad = stacked[:, :key_width]
     value_weight_grad = stacked[:, key_width:]
     normed_grad = jnp.einsum(

time: 533 us -> 460 us (0.86)
  waiting for transfers between devices: 294 us -> 185 us
  blocking collectives: 61.3 us -> 122 us
  other arithmetic: 32.8 us -> 17.6 us
  matrix products: 62.4 us -> 52.2 us
  starting transfers between devices: 8.97 us -> 15.7 us
  local copies, waits for them, and re-layouts: 57.5 us -> 52 us
    unnamed x4 -> x3, waiting for transfers between devices: 103 us -> 0.05 us
    unnamed x1, blocking collectives: 61.3 us -> 122 us
    unnamed x43, local copies, waits for them, and re-layouts: 38.6 us -> 5.64 us
    all_gather x0 -> x1, local copies, waits for them, and re-layouts: none -> 21.4 us  [body(): lax.all_gather(jnp.concatenate([key_grad_raw, value_low], axis=1), ('ctx'...]
    convert_element_type x2 -> x0, other arithmetic: 20.1 us -> none  [the longest x1 20.1 us: body(): (jnp.concatenate([key_part, value_part], axis=1) * grad_scale).astype(jnp...]
    all_gather x2 -> x3, waiting for transfers between devices: 162 us -> 155 us  [the longest x2 144 us: gather_rows(): lax.all_gather(pieces[group_index], ('ctx', 'dp', 'groups'), axis=0, tile...]
    dot_general x2 -> x1, matrix products: 16 us -> 9.91 us  [body(): jnp.einsum('btd,btk->bdk', normed_cols, grads_low, preferred_element_type...]
    all_to_all x0 -> x1, starting transfers between devices: none -> 5.46 us  [body(): normed_cols = lax.all_to_all(normed_cols, ('ctx', 'dp'), 0, 0, tiled=True)]
  transfers between devices with their start and end apart: 7 -> 8, of which waited for: 6 -> 6; matrix products, arithmetic and copies ran while one was open for 13% -> 21% of each run, Pallas kernels for 0% -> 0%
where the time goes in v2:
time: 460 us; the launch traced here: 459 us
  waiting for transfers between devices  185 us (40%)
  blocking collectives  122 us (27%)
  matrix products  52.2 us (11%)
  local copies, waits for them, and re-layouts  52 us (11%)
  other arithmetic  17.6 us (4%)
  starting transfers between devices  15.7 us (3%)
  between operations  14.8 us (3%)
    all_gather x2, waiting for transfers between devices, gather_rows(): lax.all_gather(pieces[group_index], ('ctx', 'dp', 'groups'), axis=0, tile...  144 us
    unnamed x1, blocking collectives  122 us
    ppermute x4, waiting for transfers between devices, from_behind(): lax.ppermute(value, axis, [(source, source + steps) for source in range(i...  29.7 us
    all_gather x1, local copies, waits for them, and re-layouts, body(): lax.all_gather(jnp.concatenate([key_grad_raw, value_low], axis=1), ('ctx'...  21.4 us
    dot_general x1, local copies, waits for them, and re-layouts, body(): key_raw = jnp.dot(normed, full_key, preferred_element_type=jnp.float32)  12.6 us
    all_gather x1, waiting for transfers between devices, body(): lax.all_gather(jnp.concatenate([key_grad_raw, value_low], axis=1), ('ctx'...  11.3 us
    ppermute x4, starting transfers between devices, from_behind(): lax.ppermute(value, axis, [(source, source + steps) for source in range(i...  10.1 us
    dot_general x1, matrix products, body(): jnp.einsum('btd,btk->bdk', normed_cols, grads_low, preferred_element_type...  9.91 us
  transfers between devices with their start and end apart: 8, of which 6 were waited for; matrix products, arithmetic and copies ran while one was open for 21% of the time, Pallas kernels for 0%

profile of v2, /device:TPU:0, one launch (start us, length us, event | category | flops | bytes accessed | tf_op | source)
XLA Modules:
  0.0 458.9 jit_solution(13565471771059396409)
XLA Ops:
  7.2 0.0 copy-start
  7.2 0.0 all-gather.7.cloned.1.call-start
  7.2 1.0 copy-done
  8.2 0.7 constant_dynamic-slice_fusion.1
  9.0 0.0 all-gather.7.cloned.1.call-update
  9.0 0.0 all-gather.9.cloned.1.call-start
  9.0 1.7 constant_dynamic-slice_fusion
  10.7 0.0 all-gather.9.cloned.1.call-update
  10.8 0.0 all-gather.11.cloned.1.call-start
  10.8 2.6 reshape_squeeze.7
  13.4 2.6 reshape_squeeze.6
  16.1 0.5 fusion.11
  16.6 0.3 multiply_cosine_fusion
  17.0 79.3 %all-gather.7.cloned.1.call-done = bf16[1,4608,1024]{2,1,0:T(8,128)(2,1)} async-done(((bf16[1,144,1024]{2,1,0:T(8,128)(2,1)}), bf16[1,4608,1024]{2,1,0:T(8,128)(2,1)}) %all-gather.7.cloned.1.call-update) | async-done | bytes 9437200 | tf_op jit(solution)/shard_map/all_gather | solution.py:139
  96.3 12.6 %copy.55 = bf16[1024,4608]{1,0:T(8,128)(2,1)} copy(bf16[1024,4608]{0,1:T(8,128)(2,1)} %bitcast.193) | data formatting | bytes 18874368 | tf_op jit(solution)/shard_map/dot_general | solution.py:142
  108.9 5.4 %fusion.38 = f32[256,8,128]{0,2,1:T(8,128)S(1)} fusion(bf16[8,128,4608]{2,1,0:T(8,128)(2,1)} %bitcast.194, bf16[1,256,4608]{2,1,0:T(8,128)(2,1)S(1)} %copy-done.2, f32[4608]{0:T(1024)S(1)} %copy-done.16, f32[256]{0:T(256)S(1)} %get-tuple-element.37), kind=kOutput, calls=%fused_computation.52 | convolution fusion | flops 2420637696 | bytes 12864512 | tf_op jit(solution)/shard_map/dot_general | solution.py:142
  114.3 0.2 multiply_subtract_fusion
  114.4 0.8 maximum_convert_fusion
  115.3 3.4 collective-permute-start
  118.7 64.4 %all-gather.9.cloned.1.call-done = bf16[1,4608,1024]{2,1,0:T(8,128)(2,1)} async-done(((bf16[1,144,1024]{2,1,0:T(8,128)(2,1)}), bf16[1,4608,1024]{2,1,0:T(8,128)(2,1)}) %all-gather.9.cloned.1.call-update) | async-done | bytes 9437200 | tf_op jit(solution)/shard_map/all_gather | solution.py:139
  183.1 6.3 %fusion.54 = bf16[256,1024]{1,0:T(8,128)(2,1)S(1)} fusion(bf16[1,4608,1024]{2,1,0:T(8,128)(2,1)} %all-gather.9.cloned.1.call-done, bf16[1,256,4608]{2,1,0:T(8,128)(2,1)S(1)} %copy-done.2, f32[4608]{0:T(1024)} %param.7, f32[256]{0:T(256)S(1)} %get-tuple-element.37), kind=kOutput, calls=%fused_computation.66 | convolution fusion | flops 2420899840 | bytes 12340224 | tf_op jit(solution)/shard_map/dot_general | solution.py:143
  189.4 0.0 copy-start.7
  189.4 3.7 collective-permute-start.1
  193.2 2.3 fusion.28
  195.5 0.1 copy.101
  195.6 0.7 fusion.69
  196.3 8.3 %collective-permute-done.1 = bf16[256,1024]{1,0:T(8,128)(2,1)S(1)} collective-permute-done((bf16[256,1024]{1,0:T(8,128)(2,1)S(1)}, bf16[256,1024]{1,0:T(8,128)(2,1)S(1)}, u32[]{:S(2)}, u32[]{:S(2)}) %collective-permute-start.1) | collective-permute-done | bytes 524320 | tf_op jit(solution)/shard_map/ppermute | solution.py:22
  204.5 0.1 copy.102
  204.7 1.0 fusion.29
  205.7 2.1 fusion.33
  207.9 3.2 fusion.20
  211.1 3.2 fusion.27
  214.3 0.0 copy-start.3
  214.3 0.8 fusion.63
  215.2 1.3 collective-permute-start.2
  216.5 1.6 fusion.64
  218.1 1.6 collective-permute-start.3
  219.8 12.6 %collective-permute-done.2 = bf16[256,8,128]{0,2,1:T(8,128)(2,1)S(1)} collective-permute-done((bf16[256,8,128]{0,2,1:T(8,128)(2,1)S(1)}, bf16[256,8,128]{0,2,1:T(8,128)(2,1)S(1)}, u32[]{:S(2)}, u32[]{:S(2)}) %collective-permute-start.2) | collective-permute-done | bytes 524320 | tf_op jit(solution)/shard_map/ppermute | solution.py:22
  232.4 0.8 convert_add_fusion
  233.2 0.2 add_convert_fusion.2
  233.4 8.9 %collective-permute-done.3 = bf16[256,8,128]{0,2,1:T(8,128)(2,1)S(1)} collective-permute-done((bf16[256,8,128]{0,2,1:T(8,128)(2,1)S(1)}, bf16[256,8,128]{0,2,1:T(8,128)(2,1)S(1)}, u32[]{:S(2)}, u32[]{:S(2)}) %collective-permute-start.3) | collective-permute-done | bytes 524320 | tf_op jit(solution)/shard_map/ppermute | solution.py:22
  242.3 1.6 add_convert_fusion.1
  244.0 0.8 copy-done.14
  244.7 1.0 pad_maximum_fusion
  245.8 0.0 all-gather.11.cloned.1.call-update
  245.8 3.0 copy.74
  248.8 0.1 mul.258
  248.9 3.8 fusion.34
  252.7 5.5 %all-to-all-start = ((bf16[16,256,288]{1,2,0:T(8,128)(2,1)}), bf16[16,256,288]{1,2,0:T(8,128)(2,1)}, u32[]{:S(2)}, u32[]{:S(2)}) async-start(bf16[16,256,288]{1,2,0:T(8,128)(2,1)} %fusion.34), calls=%async_computation | async-start | bytes 4718592 | tf_op jit(solution)/shard_map/all_to_all | solution.py:176
  258.2 0.6 dynamic-slice
  259.4 2.2 fusion.85
  261.6 0.0 copy-done.6
  261.6 0.1 copy-done.9
  261.7 1.4 add_convert_fusion
  263.2 2.3 copy.76
  265.4 5.3 %fusion.4 = f32[256,4608]{1,0:T(8,128)S(1)} fusion(bf16[256,1024]{0,1:T(8,128)(2,1)S(1)} %bitcast.197, bf16[1,4608,1024]{2,1,0:T(8,128)(2,1)} %all-gather.7.cloned.1.call-done), kind=kOutput, calls=%fused_computation.6 | convolution fusion | flops 2415919104 | bytes 14680064 | tf_op jit(solution)/shard_map/tk,dk->td/dot_general | solution.py:186
  270.7 9.6 %fusion.19 = (f32[4608]{0:T(1024)S(1)}, f32[256]{0:T(256)S(1)}, f32[256,4608]{1,0:T(8,128)}) fusion(bf16[1,256,4608]{2,1,0:T(8,128)(2,1)S(1)} %copy-done.2, f32[256]{0:T(256)S(1)} %get-tuple-element.37, f32[4608]{0:T(1024)S(1)} %copy-done.17, f32[256,4608]{1,0:T(8,128)S(1)} %fusion.4, bf16[256,1024]{0,1:T(8,128)(2,1)S(1)} %bitcast.205, ...), kind=kOutput, calls=%fused_computation.25 | convolution fusion | flops 2425351424 | bytes 21796864 | tf_op jit(solution)/shard_map/tk,dk->td/dot_general | solution.py:189
  280.3 121.8 %all-reduce = f32[4608]{0:T(1024)S(1)} all-reduce(f32[4608]{0:T(1024)S(1)} %broadcast_multiply_fusion), channel_id=5, replica_groups=mesh['groups'=2,'ctx'=8,'dp'=2] {'ctx','dp'}, use_global_device_ids=true, to_apply=%region_10.11.clone | all-reduce | flops 4608 | bytes 36864
  402.1 0.7 dynamic-slice.1
  402.8 5.3 %fusion.35 = bf16[1,256,4608]{2,1,0:T(8,128)(2,1)} fusion(bf16[1,256,4608]{2,1,0:T(8,128)(2,1)S(1)} %copy-done.2, f32[256,4608]{1,0:T(8,128)} %get-tuple-element.43, f32[256]{0:T(256)S(1)} %broadcast_multiply_fusion.1, f32[256]{0:T(256)S(1)} %get-tuple-element.36, f32[4608]{0:T(1024)S(1)} %copy-done.17, f32[256]{0:T(256)S(1)} %get-tuple-element.37), kind=kLoop, calls=%fused_computation.50 | loop fusion | flops 8257536 | bytes 9458688 | tf_op jit(solution)/shard_map/broadcast_in_dim | solution.py:199
  408.1 11.3 %all-gather.11.cloned.1.call-done = bf16[4096,2048]{0,1:T(8,128)(2,1)} async-done(((bf16[256,2048]{0,1:T(8,128)(2,1)}), bf16[4096,2048]{0,1:T(8,128)(2,1)}) %all-gather.11.cloned.1.call-update) | async-done | bytes 16777232 | tf_op jit(solution)/shard_map/all_gather | solution.py:177
  419.4 21.4 %copy.75 = bf16[4096,2048]{1,0:T(8,128)(2,1)} copy(bf16[4096,2048]{0,1:T(8,128)(2,1)} %all-gather.11.cloned.1.call-done) | data formatting | bytes 33554432 | tf_op jit(solution)/shard_map/all_gather | solution.py:177
  440.8 9.9 %convert_reduce_fusion = f32[288,2048]{1,0:T(8,128)S(1)} fusion(bf16[16,256,288]{1,2,0:T(8,128)(2,1)} %all-to-all-done, bf16[16,256,2048]{2,1,0:T(8,128)(2,1)} %bitcast.192), kind=kOutput, calls=%fused_computation | convolution fusion | flops 4868997120 | bytes 21495808 | tf_op jit(solution)/shard_map/btd,btk->bdk/dot_general | solution.py:180
  450.7 1.7 fusion.95
  (44 shorter events, 0.2 us)
Async XLA Ops:
  7.2 1.1 copy-start
  7.2 8.9 %copy-start.2 = (bf16[1,256,4608]{2,1,0:T(8,128)(2,1)S(1)}, bf16[1,256,4608]{2,1,0:T(8,128)(2,1)}, u32[]{:S(2)}) copy-start(bf16[1,256,4608]{2,1,0:T(8,128)(2,1)} %param.6) | copy-start | bytes 7077892
  7.2 89.1 %all-gather.7.cloned.1.call-start = ((), (), s32[]{:S(2)}) async-start(), calls=%async_computation.1 | async-start | bytes 9732096 | tf_op jit(solution)/shard_map/all_gather | solution.py:139
  9.0 174.1 %all-gather.9.cloned.1.call-start = ((), (), s32[]{:S(2)}) async-start(), calls=%async_computation.2 | async-start | bytes 9732096 | tf_op jit(solution)/shard_map/all_gather | solution.py:139
  10.8 408.6 %all-gather.11.cloned.1.call-start = ((), (), s32[]{:S(2)}) async-start(), calls=%async_computation.3 | async-start | bytes 17825792 | tf_op jit(solution)/shard_map/all_gather | solution.py:177
  16.9 97.3 %copy-start.10 = (f32[256,64]{0,1:T(8,128)}, f32[256,64]{0,1:T(8,128)S(1)}, u32[]{:S(2)}) copy-start(f32[256,64]{0,1:T(8,128)S(1)} %get-tuple-element.34) | copy-start | bytes 196612
  17.0 97.3 %copy-start.12 = (f32[256,64]{0,1:T(8,128)}, f32[256,64]{0,1:T(8,128)S(1)}, u32[]{:S(2)}) copy-start(f32[256,64]{0,1:T(8,128)S(1)} %get-tuple-element.35) | copy-start | bytes 196612
  96.3 12.6 %copy-start.16 = (f32[4608]{0:T(1024)S(1)}, f32[4608]{0:T(1024)}, u32[]{:S(2)}) copy-start(f32[4608]{0:T(1024)} %param.7) | copy-start | bytes 55300
  115.3 89.4 %collective-permute-start = (bf16[256,1024]{0,1:T(8,128)(2,1)}, bf16[256,1024]{0,1:T(8,128)(2,1)S(1)}, u32[]{:S(2)}, u32[]{:S(2)}) collective-permute-start(bf16[256,1024]{0,1:T(8,128)(2,1)} %bitcast.9), channel_id=1, source_target_pairs={{0,2},{2,4},{4,6},{6,8},{8,10},{10,12},{12,14},{1,3},{3,5},{5,7},{... | collective-permute-start | bytes 1572872 | tf_op jit(solution)/shard_map/ppermute | solution.py:22
  189.4 6.1 %copy-start.7 = (bf16[256,8,2,128]{3,2,1,0:T(2,128)(2,1)S(1)}, bf16[256,8,2,128]{3,2,1,0:T(2,128)(2,1)}, u32[]{:S(2)}) copy-start(bf16[256,8,2,128]{3,2,1,0:T(2,128)(2,1)} %reshape_squeeze.7) | copy-start | bytes 3145732
  189.4 15.1 %collective-permute-start.1 = (bf16[256,1024]{1,0:T(8,128)(2,1)S(1)}, bf16[256,1024]{1,0:T(8,128)(2,1)S(1)}, u32[]{:S(2)}, u32[]{:S(2)}) collective-permute-start(bf16[256,1024]{1,0:T(8,128)(2,1)S(1)} %fusion.54), channel_id=1, source_target_pairs={{0,2},{2,4},{4,6},{6,8},{8,10},{10,12},{12,14},{1,3},{3,5},{5,7},{... | collective-permute-start | bytes 1572872 | tf_op jit(solution)/shard_map/ppermute | solution.py:22
  195.4 9.2 %copy-start.4 = (bf16[256,8,2,128]{3,2,1,0:T(2,128)(2,1)S(1)}, bf16[256,8,2,128]{3,2,1,0:T(2,128)(2,1)}, u32[]{:S(2)}) copy-start(bf16[256,8,2,128]{3,2,1,0:T(2,128)(2,1)} %reshape_squeeze.6) | copy-start | bytes 3145732
  204.7 3.2 copy-start.8
  214.3 3.8 copy-start.5
  214.3 18.0 %copy-start.3 = (bf16[8,2,256,256]{2,3,1,0:T(8,128)(2,1)}, bf16[8,2,256,256]{2,3,1,0:T(8,128)(2,1)S(1)}, u32[]{:S(2)}) copy-start(bf16[8,2,256,256]{2,3,1,0:T(8,128)(2,1)S(1)} %get-tuple-element.32) | copy-start | bytes 6291460
  215.2 17.2 %collective-permute-start.2 = (bf16[256,8,128]{0,2,1:T(8,128)(2,1)S(1)}, bf16[256,8,128]{0,2,1:T(8,128)(2,1)S(1)}, u32[]{:S(2)}, u32[]{:S(2)}) collective-permute-start(bf16[256,8,128]{0,2,1:T(8,128)(2,1)S(1)} %fusion.63), channel_id=1, source_target_pairs={{2,0},{4,2},{6,4},{8,6},{10,8},{12,10},{14,12},{3,1},{5,3},{7,5},{... | collective-permute-start | bytes 1572872 | tf_op jit(solution)/shard_map/ppermute | solution.py:22
  218.1 15.1 %copy-start.11 = (f32[256,64]{0,1:T(8,128)S(1)}, f32[256,64]{0,1:T(8,128)}, u32[]{:S(2)}) copy-start(f32[256,64]{0,1:T(8,128)} %copy-done.10) | copy-start | bytes 196612
  218.1 15.1 %copy-start.13 = (f32[256,64]{0,1:T(8,128)S(1)}, f32[256,64]{0,1:T(8,128)}, u32[]{:S(2)}) copy-start(f32[256,64]{0,1:T(8,128)} %copy-done.12) | copy-start | bytes 196612
  218.1 24.2 %collective-permute-start.3 = (bf16[256,8,128]{0,2,1:T(8,128)(2,1)S(1)}, bf16[256,8,128]{0,2,1:T(8,128)(2,1)S(1)}, u32[]{:S(2)}, u32[]{:S(2)}) collective-permute-start(bf16[256,8,128]{0,2,1:T(8,128)(2,1)S(1)} %fusion.64), channel_id=1, source_target_pairs={{2,0},{4,2},{6,4},{8,6},{10,8},{12,10},{14,12},{3,1},{5,3},{7,5},{... | collective-permute-start | bytes 1572872 | tf_op jit(solution)/shard_map/ppermute | solution.py:22
  244.0 0.8 copy-start.14
  245.8 3.1 copy-start.17
  248.9 9.3 %copy-start.18 = (u32[32]{0:T(128)S(1)}, u32[32]{0:T(128)}, u32[]{:S(2)}) copy-start(u32[32]{0:T(128)} %constant.46) | copy-start | bytes 388
  252.7 188.1 %all-to-all-start = ((bf16[16,256,288]{1,2,0:T(8,128)(2,1)}), bf16[16,256,288]{1,2,0:T(8,128)(2,1)}, u32[]{:S(2)}, u32[]{:S(2)}) async-start(bf16[16,256,288]{1,2,0:T(8,128)(2,1)} %fusion.34), calls=%async_computation | async-start | bytes 4718592 | tf_op jit(solution)/shard_map/all_to_all | solution.py:176
  259.4 2.2 copy-start.6
  259.4 2.3 copy-start.9
  265.4 5.3 %copy-start.15 = (bf16[256,8,128]{0,2,1:T(8,128)(2,1)S(1)}, bf16[256,8,128]{0,2,1:T(8,128)(2,1)}, u32[]{:S(2)}) copy-start(bf16[256,8,128]{0,2,1:T(8,128)(2,1)} %copy-done.14) | copy-start | bytes 1572868
  440.8 11.6 %copy-start.1 = (bf16[288,1024]{1,0:T(8,128)(2,1)S(1)}, bf16[288,1024]{1,0:T(8,128)(2,1)}, u32[]{:S(2)}) copy-start(bf16[288,1024]{1,0:T(8,128)(2,1)} %param.8) | copy-start | bytes 1769476
Sparse Core Ops, SparseCore 0:
  11.5 84.7 all-gather.6
  99.8 83.2 all-gather.8
  245.9 173.4 all-gather.10

commit v3 on v2

--- a/solution.py
+++ b/solution.py
@@ -138,7 +138,19 @@
         pieces = weight.reshape(n_groups, weight.shape[0] // n_groups, weight.shape[1])
         return lax.all_gather(pieces[group_index], ("ctx", "dp", "groups"), axis=0, tiled=True)
 
-    full_key, full_value = gather_rows(key_weight), gather_rows(value_weight)
+    def exchange_gather(piece, axes):
+        count = 1
+        for axis in axes:
+            count = count * lax.axis_size(axis)
+        copies = jnp.broadcast_to(piece[None], (count,) + piece.shape)
+        return lax.all_to_all(copies, axes, 0, 0, tiled=True)
+
+    def exchange_rows(weight):
+        pieces = weight.reshape(n_groups, weight.shape[0] // n_groups, weight.shape[1])
+        gathered = exchange_gather(pieces[group_index], ("ctx", "dp", "groups"))
+        return gathered.reshape(-1, weight.shape[1])
+
+    full_key, full_value = gather_rows(key_weight), exchange_rows(value_weight)
     key_raw = jnp.dot(normed, full_key, preferred_element_type=jnp.float32)
     value_rows = jnp.dot(normed, full_value, preferred_element_type=jnp.float32).astype(
         jnp.bfloat16
@@ -174,13 +186,18 @@
     shard_rows = normed.shape[1] // n_blocks
     normed_cols = jnp.swapaxes(normed.reshape(tok_rows, n_blocks, shard_rows), 0, 1)
     normed_cols = lax.all_to_all(normed_cols, ("ctx", "dp"), 0, 0, tiled=True)
-    grads_low = lax.all_gather(
-        jnp.concatenate([key_grad_raw, value_low], axis=1), ("ctx", "dp"), axis=0
-    )
-    block_terms = jnp.einsum(
-        "btd,btk->bdk", normed_cols, grads_low, preferred_element_type=jnp.float32
-    )
-    stacked = (block_terms * grad_scale).astype(jnp.bfloat16).astype(jnp.float32).sum(0)
+    key_grads_low = lax.all_gather(key_grad_raw, ("ctx", "dp"), axis=0)
+    value_grads_low = exchange_gather(value_low, ("ctx", "dp"))
+
+    def weight_grad_rows(grads_low):
+        block_terms = jnp.einsum(
+            "btd,btk->bdk", normed_cols, grads_low, preferred_element_type=jnp.float32
+        )
+        return (block_terms * grad_scale).astype(jnp.bfloat16).astype(jnp.float32).sum(0)
+
+    stacked = jnp.concatenate(
+        [weight_grad_rows(key_grads_low), weight_grad_rows(value_grads_low)], axis=1
+    )
     key_weight_grad = stacked[:, :key_width]
     value_weight_grad = stacked[:, key_width:]
     normed_grad = jnp.einsum(
@@ -195,7 +212,10 @@
         inverse * scaled - inputs * cubed * jnp.mean(scaled * inputs, axis=-1, keepdims=True)
     ).astype(jnp.bfloat16)
     gain_term = jnp.sum(normed_grad * inputs * inverse, axis=0) * grad_scale
-    gain_grad = lax.psum_scatter(gain_term, ("ctx", "dp"), scatter_dimension=0, tiled=True)
+    gain_pieces = lax.all_to_all(
+        gain_term.reshape(n_blocks, shard_rows), ("ctx", "dp"), 0, 0, tiled=True
+    )
+    gain_grad = jnp.sum(gain_pieces, axis=0)
     return (hidden_grad[None], query_gradient[None], key_weight_grad, value_weight_grad, gain_grad)
 
 

time: 460 us -> 643 us (1.40)
  the two profiles are of different devices: /device:TPU:0 before, /device:TPU:15 now
where the time goes in v3:
time: 643 us; the launch traced here: 636 us
  waiting for transfers between devices  457 us (71%)
  matrix products  60.5 us (9%)
  starting transfers between devices  45.6 us (7%)
  local copies, waits for them, and re-layouts  39.9 us (6%)
  other arithmetic  17.8 us (3%)
  between operations  14.9 us (2%)
    all_to_all x2, waiting for transfers between devices, exchange_gather(): return lax.all_to_all(copies, axes, 0, 0, tiled=True)  184 us
    all_gather x1, waiting for transfers between devices, gather_rows(): lax.all_gather(pieces[group_index], ('ctx', 'dp', 'groups'), axis=0, tile...  130 us
    all_gather x1, waiting for transfers between devices, body(): key_grads_low = lax.all_gather(key_grad_raw, ('ctx', 'dp'), axis=0)  80.9 us
    ppermute x4, waiting for transfers between devices, from_behind(): lax.ppermute(value, axis, [(source, source + steps) for source in range(i...  59.2 us
    ppermute x4, starting transfers between devices, from_behind(): lax.ppermute(value, axis, [(source, source + steps) for source in range(i...  19.2 us
    dot_general x2, matrix products, weight_grad_rows(): jnp.einsum('btd,btk->bdk', normed_cols, grads_low, preferred_element_type...  16 us
    all_to_all x2, starting transfers between devices, exchange_gather(): return lax.all_to_all(copies, axes, 0, 0, tiled=True)  13.8 us
  transfers between devices with their start and end apart: 10, of which 7 were waited for; matrix products, arithmetic and copies ran while one was open for 17% of the time, Pallas kernels for 0%

profile of v3, /device:TPU:15, one launch (start us, length us, event | category | flops | bytes accessed | tf_op | source)
XLA Modules:
  0.0 636.0 jit_solution(15572093578903184493)
XLA Ops:
  7.2 0.0 all-gather.6.cloned.1.call-start
  7.2 1.0 copy-done
  8.2 0.7 constant_dynamic-slice_fusion
  9.0 1.0 dynamic-slice_bitcast_fusion
  10.0 4.9 broadcast_in_dim.54
  14.9 6.3 all-to-all-start
  21.2 2.7 reshape_squeeze.7
  24.0 2.6 reshape_squeeze.6
  26.6 3.1 copy.122
  29.6 0.1 mul.265
  29.8 0.5 fusion.4
  30.4 0.6 multiply_multiply_fusion
  30.9 0.3 multiply_cosine_fusion
  31.3 3.8 fusion.25
  35.1 129.8 %all-gather.6.cloned.1.call-done = bf16[1,4608,1024]{2,1,0:T(8,128)(2,1)} async-done(((bf16[1,144,1024]{2,1,0:T(8,128)(2,1)}), bf16[1,4608,1024]{2,1,0:T(8,128)(2,1)}) %all-gather.6.cloned.1.call-update) | async-done | bytes 9437200 | tf_op jit(solution)/shard_map/all_gather | solution.py:139
  164.9 12.5 %copy.103 = bf16[1024,4608]{1,0:T(8,128)(2,1)} copy(bf16[1024,4608]{0,1:T(8,128)(2,1)} %bitcast.183) | data formatting | bytes 18874368 | tf_op jit(solution)/shard_map/dot_general | solution.py:154
  177.5 5.5 fusion.27
  183.0 0.2 multiply_subtract_fusion.1
  183.1 0.8 maximum_convert_fusion
  184.0 11.5 %collective-permute-start = (bf16[256,1024]{0,1:T(8,128)(2,1)}, bf16[256,1024]{0,1:T(8,128)(2,1)S(1)}, u32[]{:S(2)}, u32[]{:S(2)}) collective-permute-start(bf16[256,1024]{0,1:T(8,128)(2,1)} %bitcast.9), channel_id=1, source_target_pairs={{0,2},{2,4},{4,6},{6,8},{8,10},{10,12},{12,14},{1,3},{3,5},{5,7},{... | collective-permute-start | bytes 1572872 | tf_op jit(solution)/shard_map/ppermute | solution.py:22
  195.5 3.0 fusion.19
  198.5 72.7 %all-to-all-done = bf16[32,144,1024]{2,1,0:T(8,128)(2,1)} async-done(((bf16[32,144,1024]{2,1,0:T(8,128)(2,1)}), bf16[32,144,1024]{2,1,0:T(8,128)(2,1)}, u32[]{:S(2)}, u32[]{:S(2)}) %all-to-all-start) | async-done | bytes 9437216 | tf_op jit(solution)/shard_map/all_to_all | solution.py:146
  271.2 7.2 %all-to-all-start.1 = ((bf16[16,256,288]{1,2,0:T(8,128)(2,1)}), bf16[16,256,288]{1,2,0:T(8,128)(2,1)}, u32[]{:S(2)}, u32[]{:S(2)}) async-start(bf16[16,256,288]{1,2,0:T(8,128)(2,1)} %fusion.25), calls=%async_computation.1 | async-start | bytes 4718592 | tf_op jit(solution)/shard_map/all_to_all | solution.py:188
  278.4 0.0 all-gather.4.cloned.1.call-start
  278.4 6.4 %fusion.41 = bf16[256,1024]{1,0:T(8,128)(2,1)S(1)} fusion(bf16[4608,1024]{1,0:T(8,128)(2,1)} %bitcast.15, bf16[1,256,4608]{2,1,0:T(8,128)(2,1)S(1)} %copy-done.2, f32[4608]{0:T(1024)} %param.7, f32[256]{0:T(256)} %copy-done.19), kind=kOutput, calls=%fused_computation.59 | convolution fusion | flops 2420899840 | bytes 12340224 | tf_op jit(solution)/shard_map/dot_general | solution.py:155
  284.9 3.4 collective-permute-start.1
  288.3 0.1 copy.152
  288.4 0.7 fusion.54
  289.2 1.0 fusion.20
  290.2 1.3 copy-done.4
  291.5 2.1 fusion.24
  293.6 1.6 fusion.49
  295.2 2.2 collective-permute-start.3
  297.4 46.9 %collective-permute-done.1 = bf16[256,1024]{1,0:T(8,128)(2,1)S(1)} collective-permute-done((bf16[256,1024]{1,0:T(8,128)(2,1)S(1)}, bf16[256,1024]{1,0:T(8,128)(2,1)S(1)}, u32[]{:S(2)}, u32[]{:S(2)}) %collective-permute-start.1) | collective-permute-done | bytes 524320 | tf_op jit(solution)/shard_map/ppermute | solution.py:22
  344.3 0.1 copy.153
  344.4 3.2 fusion.11
  347.6 3.2 fusion.18
  350.9 0.8 fusion.48
  351.7 2.1 collective-permute-start.2
  353.9 2.4 add_convert_fusion.1
  356.3 12.3 %collective-permute-done.2 = bf16[256,8,128]{0,2,1:T(8,128)(2,1)S(1)} collective-permute-done((bf16[256,8,128]{0,2,1:T(8,128)(2,1)S(1)}, bf16[256,8,128]{0,2,1:T(8,128)(2,1)S(1)}, u32[]{:S(2)}, u32[]{:S(2)}) %collective-permute-start.2) | collective-permute-done | bytes 524320 | tf_op jit(solution)/shard_map/ppermute | solution.py:22
  368.6 0.9 convert_add_fusion
  369.5 0.2 multiply_add_fusion
  369.7 1.0 copy.123
  370.7 0.0 all-gather.4.cloned.1.call-update
  370.8 5.3 fusion
  376.1 9.9 %fusion.10 = (f32[4608]{0:T(1024)S(1)}, f32[256]{0:T(256)S(1)}, f32[256,4608]{1,0:T(8,128)}) fusion(bf16[1,256,4608]{2,1,0:T(8,128)(2,1)S(1)} %copy-done.2, f32[256]{0:T(256)S(1)} %copy-done.20, f32[4608]{0:T(1024)S(1)} %copy-done.18, f32[256,4608]{1,0:T(8,128)S(1)} %fusion, bf16[256,1024]{0,1:T(8,128)(2,1)S(1)} %bitcast.192, bf16[4608,1024]{1,0:T(8,128)(2,1)} %bitcast.15), kind=kOutput, calls=%fused_computation.20 | convolution fusion | flops 2425351424 | bytes 21796864 | tf_op jit(solution)/shard_map/tk,dk->td/dot_general | solution.py:206
  386.1 0.7 mul.274
  386.8 5.3 all-to-all-start.3
  392.1 1.3 copy.124
  393.3 3.3 all-to-all-done.3
  396.7 4.3 broadcast_in_dim.56
  401.0 7.5 %all-to-all-start.2 = ((bf16[16,256,1024]{2,1,0:T(8,128)(2,1)}), bf16[16,256,1024]{2,1,0:T(8,128)(2,1)}, u32[]{:S(2)}, u32[]{:S(2)}) async-start(bf16[16,256,1024]{2,1,0:T(8,128)(2,1)} %broadcast_in_dim.56), calls=%async_computation.2 | async-start | bytes 16777216 | tf_op jit(solution)/shard_map/all_to_all | solution.py:146
  408.5 2.2 fusion.72
  410.7 0.1 copy-done.8
  410.8 0.1 copy-done.11
  410.9 1.4 add_convert_fusion
  412.3 2.3 copy.126
  414.6 5.3 fusion.26
  419.9 0.6 reduce_sum.99
  420.5 80.9 %all-gather.4.cloned.1.call-done = bf16[16,256,1024]{2,1,0:T(8,128)(2,1)} async-done(((bf16[1,256,1024]{2,1,0:T(8,128)(2,1)}), bf16[16,256,1024]{2,1,0:T(8,128)(2,1)}) %all-gather.4.cloned.1.call-update) | async-done | bytes 8388624 | tf_op jit(solution)/shard_map/all_gather | solution.py:189
  501.5 8.0 %convert_reduce_fusion.1 = f32[288,1024]{1,0:T(8,128)} fusion(bf16[16,256,288]{1,2,0:T(8,128)(2,1)} %all-to-all-done.1, bf16[16,256,1024]{2,1,0:T(8,128)(2,1)} %all-gather.4.cloned.1.call-done), kind=kOutput, calls=%fused_computation.2 | convolution fusion | flops 2434498560 | bytes 11927552 | tf_op jit(solution)/shard_map/btd,btk->bdk/dot_general | solution.py:193
  509.5 111.2 %all-to-all-done.2 = bf16[16,256,1024]{2,1,0:T(8,128)(2,1)} async-done(((bf16[16,256,1024]{2,1,0:T(8,128)(2,1)}), bf16[16,256,1024]{2,1,0:T(8,128)(2,1)}, u32[]{:S(2)}, u32[]{:S(2)}) %all-to-all-start.2) | async-done | bytes 8388640 | tf_op jit(solution)/shard_map/all_to_all | solution.py:146
  620.6 8.0 %convert_reduce_fusion = f32[288,1024]{1,0:T(8,128)} fusion(bf16[16,256,288]{1,2,0:T(8,128)(2,1)} %all-to-all-done.1, bf16[16,256,1024]{2,1,0:T(8,128)(2,1)} %all-to-all-done.2), kind=kOutput, calls=%fused_computation | convolution fusion | flops 2434498560 | bytes 11927552 | tf_op jit(solution)/shard_map/btd,btk->bdk/dot_general | solution.py:193
  (54 shorter events, 0.3 us)
Async XLA Ops:
  7.2 1.1 copy-start
  7.2 157.7 %all-gather.6.cloned.1.call-start = ((), (), s32[]{:S(2)}) async-start(), calls=%async_computation.5 | async-start | bytes 9732096 | tf_op jit(solution)/shard_map/all_gather | solution.py:139
  14.9 256.3 %all-to-all-start = ((bf16[32,144,1024]{2,1,0:T(8,128)(2,1)}), bf16[32,144,1024]{2,1,0:T(8,128)(2,1)}, u32[]{:S(2)}, u32[]{:S(2)}) async-start(bf16[32,144,1024]{2,1,0:T(8,128)(2,1)} %broadcast_in_dim.54), calls=%async_computation | async-start | bytes 18874368 | tf_op jit(solution)/shard_map/all_to_all | solution.py:146
  21.2 5.3 copy-start.2
  24.0 5.6 copy-start.17
  30.9 146.5 %copy-start.19 = (f32[256]{0:T(256)}, f32[256]{0:T(256)S(1)}, u32[]{:S(2)}) copy-start(f32[256]{0:T(256)S(1)} %get-tuple-element.45) | copy-start | bytes 3076
  31.3 151.7 %copy-start.12 = (f32[256,64]{0,1:T(8,128)}, f32[256,64]{0,1:T(8,128)S(1)}, u32[]{:S(2)}) copy-start(f32[256,64]{0,1:T(8,128)S(1)} %get-tuple-element.42) | copy-start | bytes 196612
  31.3 151.7 %copy-start.14 = (f32[256,64]{0,1:T(8,128)}, f32[256,64]{0,1:T(8,128)S(1)}, u32[]{:S(2)}) copy-start(f32[256,64]{0,1:T(8,128)S(1)} %get-tuple-element.43) | copy-start | bytes 196612
  177.5 18.0 %copy-start.5 = (bf16[256,8,2,128]{3,2,1,0:T(2,128)(2,1)S(1)}, bf16[256,8,2,128]{3,2,1,0:T(2,128)(2,1)}, u32[]{:S(2)}) copy-start(bf16[256,8,2,128]{3,2,1,0:T(2,128)(2,1)} %reshape_squeeze.6) | copy-start | bytes 3145732
  184.0 105.2 %collective-permute-start = (bf16[256,1024]{0,1:T(8,128)(2,1)}, bf16[256,1024]{0,1:T(8,128)(2,1)S(1)}, u32[]{:S(2)}, u32[]{:S(2)}) collective-permute-start(bf16[256,1024]{0,1:T(8,128)(2,1)} %bitcast.9), channel_id=1, source_target_pairs={{0,2},{2,4},{4,6},{6,8},{8,10},{10,12},{12,14},{1,3},{3,5},{5,7},{... | collective-permute-start | bytes 1572872 | tf_op jit(solution)/shard_map/ppermute | solution.py:22
  271.2 115.5 %all-to-all-start.1 = ((bf16[16,256,288]{1,2,0:T(8,128)(2,1)}), bf16[16,256,288]{1,2,0:T(8,128)(2,1)}, u32[]{:S(2)}, u32[]{:S(2)}) async-start(bf16[16,256,288]{1,2,0:T(8,128)(2,1)} %fusion.25), calls=%async_computation.1 | async-start | bytes 4718592 | tf_op jit(solution)/shard_map/all_to_all | solution.py:188
  278.4 223.1 %all-gather.4.cloned.1.call-start = ((), (), s32[]{:S(2)}) async-start(), calls=%async_computation.4 | async-start | bytes 8912896 | tf_op jit(solution)/shard_map/all_gather | solution.py:189
  278.4 10.0 %copy-start.9 = (bf16[256,8,2,128]{3,2,1,0:T(2,128)(2,1)S(1)}, bf16[256,8,2,128]{3,2,1,0:T(2,128)(2,1)}, u32[]{:S(2)}) copy-start(bf16[256,8,2,128]{3,2,1,0:T(2,128)(2,1)} %reshape_squeeze.7) | copy-start | bytes 3145732
  284.9 4.3 copy-start.6
  284.9 59.4 %collective-permute-start.1 = (bf16[256,1024]{1,0:T(8,128)(2,1)S(1)}, bf16[256,1024]{1,0:T(8,128)(2,1)S(1)}, u32[]{:S(2)}, u32[]{:S(2)}) collective-permute-start(bf16[256,1024]{1,0:T(8,128)(2,1)S(1)} %fusion.41), channel_id=1, source_target_pairs={{0,2},{2,4},{4,6},{6,8},{8,10},{10,12},{12,14},{1,3},{3,5},{5,7},{... | collective-permute-start | bytes 1572872 | tf_op jit(solution)/shard_map/ppermute | solution.py:22
  289.1 2.4 copy-start.4
  289.1 4.4 copy-start.10
  295.2 58.7 %collective-permute-start.3 = (bf16[256,8,128]{0,2,1:T(8,128)(2,1)S(1)}, bf16[256,8,128]{0,2,1:T(8,128)(2,1)S(1)}, u32[]{:S(2)}, u32[]{:S(2)}) collective-permute-start(bf16[256,8,128]{0,2,1:T(8,128)(2,1)S(1)} %fusion.49), channel_id=1, source_target_pairs={{2,0},{4,2},{6,4},{8,6},{10,8},{12,10},{14,12},{3,1},{5,3},{7,5},{... | collective-permute-start | bytes 1572872 | tf_op jit(solution)/shard_map/ppermute | solution.py:22
  350.9 5.4 copy-start.7
  350.9 17.8 %copy-start.3 = (bf16[8,2,256,256]{2,3,1,0:T(8,128)(2,1)}, bf16[8,2,256,256]{2,3,1,0:T(8,128)(2,1)S(1)}, u32[]{:S(2)}) copy-start(bf16[8,2,256,256]{2,3,1,0:T(8,128)(2,1)S(1)} %get-tuple-element.40) | copy-start | bytes 6291460
  351.7 16.9 %collective-permute-start.2 = (bf16[256,8,128]{0,2,1:T(8,128)(2,1)S(1)}, bf16[256,8,128]{0,2,1:T(8,128)(2,1)S(1)}, u32[]{:S(2)}, u32[]{:S(2)}) collective-permute-start(bf16[256,8,128]{0,2,1:T(8,128)(2,1)S(1)} %fusion.48), channel_id=1, source_target_pairs={{2,0},{4,2},{6,4},{8,6},{10,8},{12,10},{14,12},{3,1},{5,3},{7,5},{... | collective-permute-start | bytes 1572872 | tf_op jit(solution)/shard_map/ppermute | solution.py:22
  356.3 13.2 %copy-start.13 = (f32[256,64]{0,1:T(8,128)S(1)}, f32[256,64]{0,1:T(8,128)}, u32[]{:S(2)}) copy-start(f32[256,64]{0,1:T(8,128)} %copy-done.12) | copy-start | bytes 196612
  356.3 13.2 %copy-start.15 = (f32[256,64]{0,1:T(8,128)S(1)}, f32[256,64]{0,1:T(8,128)}, u32[]{:S(2)}) copy-start(f32[256,64]{0,1:T(8,128)} %copy-done.14) | copy-start | bytes 196612
  370.8 5.3 copy-start.16
  370.8 5.3 copy-start.18
  370.8 5.3 copy-start.20
  386.8 9.9 %all-to-all-start.3 = ((f32[16,1,288]{2,1,0:T(1,128)}), f32[16,1,288]{2,1,0:T(1,128)S(1)}, u32[]{:S(2)}, u32[]{:S(2)}) async-start(f32[16,1,288]{2,1,0:T(1,128)} %mul.274), calls=%async_computation.3 | async-start | bytes 49152 | tf_op jit(solution)/shard_map/all_to_all | solution.py:215
  401.0 219.7 %all-to-all-start.2 = ((bf16[16,256,1024]{2,1,0:T(8,128)(2,1)}), bf16[16,256,1024]{2,1,0:T(8,128)(2,1)}, u32[]{:S(2)}, u32[]{:S(2)}) async-start(bf16[16,256,1024]{2,1,0:T(8,128)(2,1)} %broadcast_in_dim.56), calls=%async_computation.2 | async-start | bytes 16777216 | tf_op jit(solution)/shard_map/all_to_all | solution.py:146
  408.5 2.3 copy-start.8
  408.5 2.4 copy-start.11
  410.9 3.7 copy-start.21
  620.6 8.0 %copy-start.1 = (bf16[288,1024]{1,0:T(8,128)(2,1)S(1)}, bf16[288,1024]{1,0:T(8,128)(2,1)}, u32[]{:S(2)}) copy-start(bf16[288,1024]{1,0:T(8,128)(2,1)} %param.8) | copy-start | bytes 1769476
Sparse Core Ops, SparseCore 0:
  11.5 153.3 all-gather.5
  370.9 130.5 all-gather.3

commit v4 on v2

--- a/solution.py
+++ b/solution.py
@@ -125,24 +125,61 @@
     return (query_out, nearby_key, nearby_value, distant_key, distant_value)
 
 
+def ring_order(n_ctx, n_dp):
+    if n_ctx % 2 == 0:
+        half = n_ctx // 2
+        chips = [2 * a for a in range(half)] + [2 * a + 1 for a in reversed(range(half))]
+    else:
+        chips = list(range(n_ctx))
+    return [chip * n_dp + core for chip in chips for core in range(n_dp)]
+
+
+def ring_gather(piece, axes, ring):
+    count = len(ring)
+    ahead = [(ring[i], ring[(i + 1) % count]) for i in range(count)]
+    behind = [(ring[i], ring[(i - 1) % count]) for i in range(count)]
+    n_ahead = count // 2
+    from_left, from_right = [], []
+    moving = piece
+    for _ in range(n_ahead):
+        moving = lax.ppermute(moving, axes, ahead)
+        from_left.append(moving)
+    moving = piece
+    for _ in range(count - 1 - n_ahead):
+        moving = lax.ppermute(moving, axes, behind)
+        from_right.append(moving)
+    return jnp.stack([piece] + from_right + from_left[::-1])
+
+
 def body(hidden_in, norm_gain, key_weight, value_weight, queries, out_grad):
     tok_rows = hidden_in.shape[1]
     key_width = key_weight.shape[1]
     inputs = hidden_in[0].astype(jnp.float32)
     inverse = lax.rsqrt(jnp.mean(inputs * inputs, axis=-1, keepdims=True) + norm_eps)
     normed = (inputs * inverse * norm_gain).astype(jnp.bfloat16)
-    n_groups = lax.axis_size("groups")
-    group_index = lax.axis_index("groups")
-
-    def gather_rows(weight):
-        pieces = weight.reshape(n_groups, weight.shape[0] // n_groups, weight.shape[1])
-        return lax.all_gather(pieces[group_index], ("ctx", "dp", "groups"), axis=0, tiled=True)
-
-    full_key, full_value = gather_rows(key_weight), gather_rows(value_weight)
-    key_raw = jnp.dot(normed, full_key, preferred_element_type=jnp.float32)
-    value_rows = jnp.dot(normed, full_value, preferred_element_type=jnp.float32).astype(
-        jnp.bfloat16
-    )
+    n_ctx = lax.axis_size("ctx")
+    n_dp = lax.axis_size("dp")
+    n_blocks = n_ctx * n_dp
+    shard_rows = normed.shape[1] // n_blocks
+    ring = ring_order(n_ctx, n_dp)
+    ring_pos = [0] * n_blocks
+    for place, member in enumerate(ring):
+        ring_pos[member] = place
+    my_place = jnp.array(ring_pos, jnp.int32)[lax.axis_index("ctx") * n_dp + lax.axis_index("dp")]
+    offsets = jnp.arange(n_blocks, dtype=jnp.int32)
+    source_of = jnp.array(ring, jnp.int32)[(my_place + offsets) % n_blocks]
+    offset_of = (jnp.array(ring_pos, jnp.int32) - my_place) % n_blocks
+    weights = ring_gather(
+        jnp.concatenate([key_weight, value_weight], axis=1), ("ctx", "dp"), ring
+    )
+    full_key, full_value = weights[..., :key_width], weights[..., key_width:]
+    normed_blocks = jnp.take(normed.reshape(tok_rows, n_blocks, shard_rows), source_of, axis=1)
+    key_raw = jnp.einsum(
+        "tjr,jrk->tk", normed_blocks, full_key, preferred_element_type=jnp.float32
+    )
+    value_rows = jnp.einsum(
+        "tjr,jrk->tk", normed_blocks, full_value, preferred_element_type=jnp.float32
+    ).astype(jnp.bfloat16)
     ctx_index = lax.axis_index("ctx")
     positions = ctx_index * tok_rows + jnp.arange(tok_rows, dtype=jnp.int32)
     cosine_table, sine_table = rotation(positions)
@@ -170,12 +207,11 @@
         .reshape(tok_rows, key_width)
     )
     value_low = value_grad.astype(jnp.bfloat16).reshape(tok_rows, key_width)
-    n_blocks = lax.axis_size("ctx") * lax.axis_size("dp")
-    shard_rows = normed.shape[1] // n_blocks
     normed_cols = jnp.swapaxes(normed.reshape(tok_rows, n_blocks, shard_rows), 0, 1)
     normed_cols = lax.all_to_all(normed_cols, ("ctx", "dp"), 0, 0, tiled=True)
-    grads_low = lax.all_gather(
-        jnp.concatenate([key_grad_raw, value_low], axis=1), ("ctx", "dp"), axis=0
+    normed_cols = jnp.take(normed_cols, source_of, axis=0)
+    grads_low = ring_gather(
+        jnp.concatenate([key_grad_raw, value_low], axis=1), ("ctx", "dp"), ring
     )
     block_terms = jnp.einsum(
         "btd,btk->bdk", normed_cols, grads_low, preferred_element_type=jnp.float32
@@ -184,18 +220,22 @@
     key_weight_grad = stacked[:, :key_width]
     value_weight_grad = stacked[:, key_width:]
     normed_grad = jnp.einsum(
-        "tk,dk->td", key_grad_raw, full_key, preferred_element_type=jnp.float32
+        "tk,jrk->tjr", key_grad_raw, full_key, preferred_element_type=jnp.float32
     )
     normed_grad = normed_grad + jnp.einsum(
-        "tk,dk->td", value_low, full_value, preferred_element_type=jnp.float32
-    )
+        "tk,jrk->tjr", value_low, full_value, preferred_element_type=jnp.float32
+    )
+    normed_grad = jnp.take(normed_grad, offset_of, axis=1).reshape(tok_rows, -1)
     scaled = normed_grad * norm_gain
     cubed = inverse * inverse * inverse
     hidden_grad = (
         inverse * scaled - inputs * cubed * jnp.mean(scaled * inputs, axis=-1, keepdims=True)
     ).astype(jnp.bfloat16)
     gain_term = jnp.sum(normed_grad * inputs * inverse, axis=0) * grad_scale
-    gain_grad = lax.psum_scatter(gain_term, ("ctx", "dp"), scatter_dimension=0, tiled=True)
+    gain_pieces = lax.all_to_all(
+        gain_term.reshape(n_blocks, shard_rows), ("ctx", "dp"), 0, 0, tiled=True
+    )
+    gain_grad = jnp.sum(gain_pieces, axis=0)
     return (hidden_grad[None], query_gradient[None], key_weight_grad, value_weight_grad, gain_grad)
 
 

time: 460 us -> 440 us (0.957); the launches traced: 459 us -> 434 us
  blocking collectives: 122 us -> 0 us
  starting transfers between devices: 15.7 us -> 103 us
  local copies, waits for them, and re-layouts: 52 us -> 85.8 us
  waiting for transfers between devices: 185 us -> 158 us
  other arithmetic: 17.6 us -> 32.9 us
  between operations: 14.8 us -> 1.67 us
    all_gather x3 -> x0, waiting for transfers between devices: 155 us -> none  [the longest x2 144 us: gather_rows(): lax.all_gather(pieces[group_index], ('ctx', 'dp', 'groups'), axis=0, tile...]
    ppermute x0 -> x30, waiting for transfers between devices: none -> 124 us  [the longest x16 102 us: ring_gather(): moving = lax.ppermute(moving, axes, ahead)]
    unnamed x1 -> x0, blocking collectives: 122 us -> none
    ppermute x0 -> x30, starting transfers between devices: none -> 64.3 us  [the longest x16 45.1 us: ring_gather(): moving = lax.ppermute(moving, axes, ahead)]
    unnamed x43 -> x120, local copies, waits for them, and re-layouts: 5.64 us -> 57.4 us
    all_gather x1 -> x0, local copies, waits for them, and re-layouts: 21.4 us -> none  [body(): lax.all_gather(jnp.concatenate([key_grad_raw, value_low], axis=1), ('ctx'...]
    gather x0 -> x4, local copies, waits for them, and re-layouts: none -> 13.7 us  [the longest x1 5.38 us: body(): normed_grad = jnp.take(normed_grad, offset_of, axis=1).reshape(tok_rows, -1)]
    dot_general x1 -> x0, local copies, waits for them, and re-layouts: 12.6 us -> none  [body(): key_raw = jnp.dot(normed, full_key, preferred_element_type=jnp.float32)]
  transfers between devices with their start and end apart: 8 -> 36, of which waited for: 6 -> 20; matrix products, arithmetic and copies ran while one was open for 21% -> 31% of each run, Pallas kernels for 0% -> 0%
where the time goes in v4:
time: 440 us; the launch traced here: 434 us
  waiting for transfers between devices  158 us (36%)
  starting transfers between devices  103 us (23%)
  local copies, waits for them, and re-layouts  85.8 us (20%)
  matrix products  51.9 us (12%)
  other arithmetic  32.9 us (7%)
    ppermute x16, waiting for transfers between devices, ring_gather(): moving = lax.ppermute(moving, axes, ahead)  102 us
    unnamed x120, local copies, waits for them, and re-layouts  57.4 us
    ppermute x16, starting transfers between devices, ring_gather(): moving = lax.ppermute(moving, axes, ahead)  45.1 us
    ppermute x4, waiting for transfers between devices, from_behind(): lax.ppermute(value, axis, [(source, source + steps) for source in range(i...  34.1 us
    ppermute x4, starting transfers between devices, from_behind(): lax.ppermute(value, axis, [(source, source + steps) for source in range(i...  22.6 us
    ppermute x14, waiting for transfers between devices, ring_gather(): moving = lax.ppermute(moving, axes, behind)  21.5 us
    ppermute x14, starting transfers between devices, ring_gather(): moving = lax.ppermute(moving, axes, behind)  19.1 us
    dot_general x1, matrix products, body(): jnp.einsum('btd,btk->bdk', normed_cols, grads_low, preferred_element_type...  12.8 us
  transfers between devices with their start and end apart: 36, of which 20 were waited for; matrix products, arithmetic and copies ran while one was open for 31% of the time, Pallas kernels for 0%

profile of v4, /device:TPU:0, one launch (start us, length us, event | category | flops | bytes accessed | tf_op | source)
XLA Modules:
  0.0 433.6 jit_solution(8273650194479461994)
XLA Ops:
  3.4 2.0 collective-permute-start
  5.4 13.8 %collective-permute-done.7 = bf16[288,2048]{1,0:T(8,128)(2,1)S(1)} collective-permute-done((bf16[288,2048]{1,0:T(8,128)(2,1)S(1)}, bf16[288,2048]{1,0:T(8,128)(2,1)S(1)}, u32[]{:S(2)}, u32[]{:S(2)}) %collective-permute-start.7) | collective-permute-done | bytes 1179680 | tf_op jit(solution)/shard_map/ppermute | solution.py:145
  19.2 2.0 collective-permute-start.1
  21.2 13.6 %collective-permute-done.8 = bf16[288,2048]{1,0:T(8,128)(2,1)S(1)} collective-permute-done((bf16[288,2048]{1,0:T(8,128)(2,1)S(1)}, bf16[288,2048]{1,0:T(8,128)(2,1)S(1)}, u32[]{:S(2)}, u32[]{:S(2)}) %collective-permute-start.8) | collective-permute-done | bytes 1179680 | tf_op jit(solution)/shard_map/ppermute | solution.py:145
  35.0 2.0 collective-permute-start.2
  37.0 13.5 %collective-permute-done.9 = bf16[288,2048]{1,0:T(8,128)(2,1)S(1)} collective-permute-done((bf16[288,2048]{1,0:T(8,128)(2,1)S(1)}, bf16[288,2048]{1,0:T(8,128)(2,1)S(1)}, u32[]{:S(2)}, u32[]{:S(2)}) %collective-permute-start.9) | collective-permute-done | bytes 1179680 | tf_op jit(solution)/shard_map/ppermute | solution.py:145
  50.6 3.2 copy.95
  57.8 2.6 fusion.110
  60.4 6.8 %all-to-all-start = ((bf16[16,256,288]{1,2,0:T(8,128)(2,1)}), bf16[16,256,288]{1,2,0:T(8,128)(2,1)}, u32[]{:S(2)}, u32[]{:S(2)}) async-start(bf16[16,256,288]{1,2,0:T(8,128)(2,1)} %fusion.110), calls=%async_computation | async-start | bytes 4718592 | tf_op jit(solution)/shard_map/all_to_all | solution.py:211
  71.3 4.1 collective-permute-done.3
  75.5 2.0 collective-permute-start.4
  78.2 2.5 multiply_convert_fusion.1
  80.7 21.3 %collective-permute-done.11 = bf16[288,2048]{1,0:T(8,128)(2,1)} collective-permute-done((bf16[288,2048]{1,0:T(8,128)(2,1)}, bf16[288,2048]{1,0:T(8,128)(2,1)}, u32[]{:S(2)}, u32[]{:S(2)}) %collective-permute-start.11) | collective-permute-done | bytes 1179680 | tf_op jit(solution)/shard_map/ppermute | solution.py:145
  101.9 17.8 %collective-permute-start.12 = (bf16[288,2048]{1,0:T(8,128)(2,1)}, bf16[288,2048]{1,0:T(8,128)(2,1)}, u32[]{:S(2)}, u32[]{:S(2)}) collective-permute-start(bf16[288,2048]{1,0:T(8,128)(2,1)} %collective-permute-done.11), channel_id=1, source_target_pairs={{0,1},{1,4},{4,5},{5,8},{8,9},{9,12},{12,13},{13,14},{14,15},{15,1... | collective-permute-start | bytes 3538952 | tf_op jit(solution)/shard_map/ppermute | solution.py:145
  123.1 3.8 gather_fusion.1
  130.2 5.4 %collective-permute-start.13 = (bf16[288,2048]{1,0:T(8,128)(2,1)}, bf16[288,2048]{1,0:T(8,128)(2,1)S(1)}, u32[]{:S(2)}, u32[]{:S(2)}) collective-permute-start(bf16[288,2048]{1,0:T(8,128)(2,1)} %collective-permute-done.12), channel_id=1, source_target_pairs={{0,1},{1,4},{4,5},{5,8},{8,9},{9,12},{12,13},{13,14},{14,15},{15,1... | collective-permute-start | bytes 3538952 | tf_op jit(solution)/shard_map/ppermute | solution.py:145
  138.3 4.6 %collective-permute-done.5 = bf16[288,2048]{1,0:T(8,128)(2,1)S(1)} collective-permute-done((bf16[288,2048]{1,0:T(8,128)(2,1)}, bf16[288,2048]{1,0:T(8,128)(2,1)S(1)}, u32[]{:S(2)}, u32[]{:S(2)}) %collective-permute-start.5) | collective-permute-done | bytes 1179680 | tf_op jit(solution)/shard_map/ppermute | solution.py:149
  147.4 12.4 %collective-permute-start.14 = (bf16[288,2048]{1,0:T(8,128)(2,1)S(1)}, bf16[288,2048]{1,0:T(8,128)(2,1)S(1)}, u32[]{:S(2)}, u32[]{:S(2)}) collective-permute-start(bf16[288,2048]{1,0:T(8,128)(2,1)S(1)} %collective-permute-done.13), channel_id=1, source_target_pairs={{0,1},{1,4},{4,5},{5,8},{8,9},{9,12},{12,13},{13,14},{14,15},{15,1... | collective-permute-start | bytes 3538952 | tf_op jit(solution)/shard_map/ppermute | solution.py:145
  168.5 2.7 fusion.40
  171.2 3.7 copy-done.7
  174.9 3.5 fusion.50
  180.9 2.0 copy.99
  182.9 16.8 %collective-permute-start.15 = (bf16[256,1024]{0,1:T(8,128)(2,1)}, bf16[256,1024]{0,1:T(8,128)(2,1)S(1)}, u32[]{:S(2)}, u32[]{:S(2)}) collective-permute-start(bf16[256,1024]{0,1:T(8,128)(2,1)} %bitcast.256), channel_id=1, source_target_pairs={{0,2},{2,4},{4,6},{6,8},{8,10},{10,12},{12,14},{1,3},{3,5},{5,7},{... | collective-permute-start | bytes 1572872 | tf_op jit(solution)/shard_map/ppermute | solution.py:22
  199.7 2.7 collective-permute-start.16
  203.6 1.9 fusion.66
  206.5 12.4 %collective-permute-done.16 = bf16[256,1024]{1,0:T(8,128)(2,1)S(1)} collective-permute-done((bf16[256,1024]{1,0:T(8,128)(2,1)}, bf16[256,1024]{1,0:T(8,128)(2,1)S(1)}, u32[]{:S(2)}, u32[]{:S(2)}) %collective-permute-start.16) | collective-permute-done | bytes 524320 | tf_op jit(solution)/shard_map/ppermute | solution.py:22
  220.2 2.1 fusion.22
  222.3 3.2 fusion.9
  225.6 3.2 fusion.16
  230.9 2.4 fusion.60
  235.1 12.0 %collective-permute-done.17 = bf16[256,8,128]{2,0,1:T(8,128)(2,1)S(1)} collective-permute-done((bf16[256,8,128]{2,0,1:T(8,128)(2,1)S(1)}, bf16[256,8,128]{2,0,1:T(8,128)(2,1)S(1)}, u32[]{:S(2)}, u32[]{:S(2)}) %collective-permute-start.17) | collective-permute-done | bytes 524320 | tf_op jit(solution)/shard_map/ppermute | solution.py:22
  248.8 9.6 %collective-permute-done.18 = bf16[256,8,128]{0,2,1:T(8,128)(2,1)} collective-permute-done((bf16[256,8,128]{0,2,1:T(8,128)(2,1)}, bf16[256,8,128]{0,2,1:T(8,128)(2,1)}, u32[]{:S(2)}, u32[]{:S(2)}) %collective-permute-start.18) | collective-permute-done | bytes 524320 | tf_op jit(solution)/shard_map/ppermute | solution.py:22
  258.4 4.3 add_convert_fusion.1
  268.7 12.4 %collective-permute-done.26 = bf16[256,2048]{1,0:T(8,128)(2,1)S(1)} collective-permute-done((bf16[256,2048]{1,0:T(8,128)(2,1)S(1)}, bf16[256,2048]{1,0:T(8,128)(2,1)S(1)}, u32[]{:S(2)}, u32[]{:S(2)}) %collective-permute-start.26) | collective-permute-done | bytes 1048608 | tf_op jit(solution)/shard_map/ppermute | solution.py:145
  284.0 12.4 %collective-permute-done.27 = bf16[256,2048]{1,0:T(8,128)(2,1)} collective-permute-done((bf16[256,2048]{1,0:T(8,128)(2,1)S(1)}, bf16[256,2048]{1,0:T(8,128)(2,1)}, u32[]{:S(2)}, u32[]{:S(2)}) %collective-permute-start.27) | collective-permute-done | bytes 1048608 | tf_op jit(solution)/shard_map/ppermute | solution.py:145
  299.1 3.9 gather_fusion.3
  303.0 2.2 fusion.82
  305.4 5.6 %collective-permute-done.28 = bf16[256,2048]{1,0:T(8,128)(2,1)} collective-permute-done((bf16[256,2048]{1,0:T(8,128)(2,1)}, bf16[256,2048]{1,0:T(8,128)(2,1)}, u32[]{:S(2)}, u32[]{:S(2)}) %collective-permute-start.28) | collective-permute-done | bytes 1048608 | tf_op jit(solution)/shard_map/ppermute | solution.py:145
  311.0 1.9 collective-permute-start.29
  314.3 2.3 copy.124
  316.6 5.3 %fusion = f32[256,16,288]{0,2,1:T(8,128)S(1)} fusion(bf16[256,1024,1]{0,1,2:T(8,128)(2,1)S(1)} %bitcast.253, bf16[16,288,2048]{2,1,0:T(8,128)(2,1)} %copy-done.7), kind=kOutput, calls=%fused_computation.6 | convolution fusion | flops 2415919104 | bytes 14680064 | tf_op jit(solution)/shard_map/tk,jrk->tjr/dot_general | solution.py:225
  322.0 3.5 collective-permute-done.29
  325.5 1.9 collective-permute-start.30
  327.4 8.5 %fusion.27 = f32[256,16,288]{0,2,1:T(8,128)} fusion(f32[256,16,288]{0,2,1:T(8,128)S(1)} %fusion, bf16[256,1024,1]{0,1,2:T(8,128)(2,1)S(1)} %bitcast.247, bf16[16,288,2048]{2,1,0:T(8,128)(2,1)} %copy-done.7), kind=kOutput, calls=%fused_computation.48 | convolution fusion | flops 2417098752 | bytes 19398656 | tf_op jit(solution)/shard_map/tk,jrk->tjr/dot_general | solution.py:222
  336.0 5.4 %gather_fusion.2 = f32[16,256,288]{1,2,0:T(8,128)} fusion(f32[256,16,288]{0,2,1:T(8,128)} %fusion.27, s32[1024]{0:T(1024)S(1)} %pad_clamp_fusion), kind=kCustom, calls=%fused_computation.2 | custom fusion | bytes 9437248 | tf_op jit(solution)/shard_map/jit(_take)/gather | solution.py:228
  341.4 5.4 %multiply_reduce_fusion = (f32[4608]{0:T(1024)S(1)}, f32[256]{0:T(256)S(1)}) fusion(bf16[1,256,4608]{1,2,0:T(8,128)(2,1)S(1)} %copy.95, f32[256]{0:T(256)S(1)} %copy-done.35, pred[4608]{0:T(1024)(128)(4,1)S(1)} %broadcast_in_dim.73, f32[4608]{0:T(1024)S(1)} %copy-done.32, f32[1,256,4608]{1,2,0:T(8,128)} %bitcast.243), kind=kLoop, calls=%fused_computation.15 | loop fusion | flops 9432320 | bytes 7121408 | tf_op jit(solution)/shard_map/reduce_sum | solution.py:234
  347.5 9.7 %all-to-all-start.1 = ((f32[16,1,288]{2,1,0:T(1,128)}), f32[16,1,288]{2,1,0:T(1,128)S(1)}, u32[]{:S(2)}, u32[]{:S(2)}) async-start(f32[16,1,288]{2,1,0:T(1,128)} %mul.289), calls=%async_computation.1 | async-start | bytes 49152 | tf_op jit(solution)/shard_map/all_to_all | solution.py:235
  359.2 6.0 %subtract_convert_fusion = bf16[1,256,4608]{1,2,0:T(8,128)(2,1)} fusion(bf16[1,256,4608]{1,2,0:T(8,128)(2,1)S(1)} %copy.95, f32[256]{0:T(256)S(1)} %broadcast_multiply_fusion.1, f32[256]{0:T(256)S(1)} %copy-done.37, f32[4608]{0:T(1024)S(1)} %copy-done.32, f32[256]{0:T(256)S(1)} %copy-done.35, pred[4608]{0:T(1024)(128)(4,1)S(1)} %broadcast_in_dim.73, ...), kind=kLoop, calls=%fused_computation.16 | loop fusion | flops 9437184 | bytes 9463296 | tf_op jit(solution)/shard_map/convert_element_type | solution.py:233
  366.4 4.3 copy.123
  371.8 2.1 collective-permute-start.24
  373.9 2.3 bitcast_dynamic-update-slice_fusion.30
  376.2 2.3 bitcast_dynamic-update-slice_fusion.29
  378.5 2.3 bitcast_dynamic-update-slice_fusion.28
  380.8 5.7 %collective-permute-done.24 = bf16[256,2048]{1,0:T(8,128)(2,1)S(1)} collective-permute-done((bf16[256,2048]{1,0:T(8,128)(2,1)}, bf16[256,2048]{1,0:T(8,128)(2,1)S(1)}, u32[]{:S(2)}, u32[]{:S(2)}) %collective-permute-start.24) | collective-permute-done | bytes 1048608 | tf_op jit(solution)/shard_map/ppermute | solution.py:149
  386.5 2.1 collective-permute-start.25
  388.6 2.4 bitcast_dynamic-update-slice_fusion.27
  390.9 2.3 bitcast_dynamic-update-slice_fusion.26
  394.4 6.5 %collective-permute-done.25 = bf16[256,2048]{1,0:T(8,128)(2,1)S(1)} collective-permute-done((bf16[256,2048]{1,0:T(8,128)(2,1)S(1)}, bf16[256,2048]{1,0:T(8,128)(2,1)S(1)}, u32[]{:S(2)}, u32[]{:S(2)}) %collective-permute-start.25) | collective-permute-done | bytes 1048608 | tf_op jit(solution)/shard_map/ppermute | solution.py:149
  402.0 3.1 collective-permute-done.33
  408.3 2.5 bitcast_dynamic-update-slice_fusion.20
  410.8 2.5 bitcast_dynamic-update-slice_fusion.19
  413.2 2.3 bitcast_dynamic-update-slice_fusion.18
  415.6 2.3 bitcast_dynamic-update-slice_fusion.17
  419.0 12.8 %convert_reduce_fusion = f32[288,2048]{1,0:T(8,128)S(1)} fusion(bf16[16,256,2048]{2,1,0:T(8,128)(2,1)} %bitcast_dynamic-update-slice_fusion.16, bf16[16,256,288]{1,2,0:T(8,128)(2,1)S(1)} %copy-done.10, pred[16]{0:T(512)(128)(4,1)S(1)} %copy-done.41), kind=kOutput, calls=%fused_computation.4 | convolution fusion | flops 4870176768 | bytes 21495824 | tf_op jit(solution)/shard_map/btd,btk->bdk/dot_general | solution.py:216
  (195 shorter events, 71.3 us)
Async XLA Ops:
  2.9 47.6 %copy-start.13 = (bf16[288,2048]{1,0:T(8,128)(2,1)}, bf16[288,2048]{1,0:T(8,128)(2,1)S(1)}, u32[]{:S(2)}) copy-start(bf16[288,2048]{1,0:T(8,128)(2,1)S(1)} %constant_dynamic-update-slice_fusion) | copy-start | bytes 3538948
  2.9 16.3 %collective-permute-start.7 = (bf16[288,2048]{1,0:T(8,128)(2,1)S(1)}, bf16[288,2048]{1,0:T(8,128)(2,1)S(1)}, u32[]{:S(2)}, u32[]{:S(2)}) collective-permute-start(bf16[288,2048]{1,0:T(8,128)(2,1)S(1)} %constant_dynamic-update-slice_fusion), channel_id=1, source_target_pairs={{0,1},{1,4},{4,5},{5,8},{8,9},{9,12},{12,13},{13,14},{14,15},{15,1... | collective-permute-start | bytes 3538952 | tf_op jit(solution)/shard_map/ppermute | solution.py:145
  3.4 15.8 %collective-permute-start = (bf16[288,2048]{1,0:T(8,128)(2,1)S(1)}, bf16[288,2048]{1,0:T(8,128)(2,1)S(1)}, u32[]{:S(2)}, u32[]{:S(2)}) collective-permute-start(bf16[288,2048]{1,0:T(8,128)(2,1)S(1)} %constant_dynamic-update-slice_fusion), channel_id=1, source_target_pairs={{0,3},{1,0},{4,1},{5,4},{8,5},{9,8},{12,9},{13,12},{14,13},{15,14}... | collective-permute-start | bytes 3538952 | tf_op jit(solution)/shard_map/ppermute | solution.py:149
  19.2 31.3 %copy-start.16 = (bf16[288,2048]{1,0:T(8,128)(2,1)}, bf16[288,2048]{1,0:T(8,128)(2,1)S(1)}, u32[]{:S(2)}) copy-start(bf16[288,2048]{1,0:T(8,128)(2,1)S(1)} %collective-permute-done.7) | copy-start | bytes 3538948
  19.2 15.6 %collective-permute-start.8 = (bf16[288,2048]{1,0:T(8,128)(2,1)S(1)}, bf16[288,2048]{1,0:T(8,128)(2,1)S(1)}, u32[]{:S(2)}, u32[]{:S(2)}) collective-permute-start(bf16[288,2048]{1,0:T(8,128)(2,1)S(1)} %collective-permute-done.7), channel_id=1, source_target_pairs={{0,1},{1,4},{4,5},{5,8},{8,9},{9,12},{12,13},{13,14},{14,15},{15,1... | collective-permute-start | bytes 3538952 | tf_op jit(solution)/shard_map/ppermute | solution.py:145
  19.2 31.3 %copy-start.22 = (bf16[288,2048]{1,0:T(8,128)(2,1)}, bf16[288,2048]{1,0:T(8,128)(2,1)S(1)}, u32[]{:S(2)}) copy-start(bf16[288,2048]{1,0:T(8,128)(2,1)S(1)} %collective-permute-done) | copy-start | bytes 3538948
  19.2 15.7 %collective-permute-start.1 = (bf16[288,2048]{1,0:T(8,128)(2,1)S(1)}, bf16[288,2048]{1,0:T(8,128)(2,1)}, u32[]{:S(2)}, u32[]{:S(2)}) collective-permute-start(bf16[288,2048]{1,0:T(8,128)(2,1)S(1)} %collective-permute-done), channel_id=1, source_target_pairs={{0,3},{1,0},{4,1},{5,4},{8,5},{9,8},{12,9},{13,12},{14,13},{15,14}... | collective-permute-start | bytes 3538952 | tf_op jit(solution)/shard_map/ppermute | solution.py:149
  34.8 15.6 %copy-start.18 = (bf16[288,2048]{1,0:T(8,128)(2,1)}, bf16[288,2048]{1,0:T(8,128)(2,1)S(1)}, u32[]{:S(2)}) copy-start(bf16[288,2048]{1,0:T(8,128)(2,1)S(1)} %collective-permute-done.8) | copy-start | bytes 3538948
  34.9 15.6 %collective-permute-start.9 = (bf16[288,2048]{1,0:T(8,128)(2,1)S(1)}, bf16[288,2048]{1,0:T(8,128)(2,1)S(1)}, u32[]{:S(2)}, u32[]{:S(2)}) collective-permute-start(bf16[288,2048]{1,0:T(8,128)(2,1)S(1)} %collective-permute-done.8), channel_id=1, source_target_pairs={{0,1},{1,4},{4,5},{5,8},{8,9},{9,12},{12,13},{13,14},{14,15},{15,1... | collective-permute-start | bytes 3538952 | tf_op jit(solution)/shard_map/ppermute | solution.py:145
  35.0 21.5 %collective-permute-start.2 = (bf16[288,2048]{1,0:T(8,128)(2,1)}, bf16[288,2048]{1,0:T(8,128)(2,1)}, u32[]{:S(2)}, u32[]{:S(2)}) collective-permute-start(bf16[288,2048]{1,0:T(8,128)(2,1)} %collective-permute-done.1), channel_id=1, source_target_pairs={{0,3},{1,0},{4,1},{5,4},{8,5},{9,8},{12,9},{13,12},{14,13},{15,14}... | collective-permute-start | bytes 3538952 | tf_op jit(solution)/shard_map/ppermute | solution.py:149
  50.5 9.9 %copy-start.20 = (bf16[288,2048]{1,0:T(8,128)(2,1)}, bf16[288,2048]{1,0:T(8,128)(2,1)S(1)}, u32[]{:S(2)}) copy-start(bf16[288,2048]{1,0:T(8,128)(2,1)S(1)} %collective-permute-done.9) | copy-start | bytes 3538948
  50.5 18.0 %collective-permute-start.10 = (bf16[288,2048]{1,0:T(8,128)(2,1)S(1)}, bf16[288,2048]{1,0:T(8,128)(2,1)}, u32[]{:S(2)}, u32[]{:S(2)}) collective-permute-start(bf16[288,2048]{1,0:T(8,128)(2,1)S(1)} %collective-permute-done.9), channel_id=1, source_target_pairs={{0,1},{1,4},{4,5},{5,8},{8,9},{9,12},{12,13},{13,14},{14,15},{15,1... | collective-permute-start | bytes 3538952 | tf_op jit(solution)/shard_map/ppermute | solution.py:145
  56.4 21.8 %copy-start.34 = (f32[256]{0:T(256)}, f32[256]{0:T(256)S(1)}, u32[]{:S(2)}) copy-start(f32[256]{0:T(256)S(1)} %get-tuple-element.46) | copy-start | bytes 3076
  56.4 19.0 %collective-permute-start.3 = (bf16[288,2048]{1,0:T(8,128)(2,1)}, bf16[288,2048]{1,0:T(8,128)(2,1)}, u32[]{:S(2)}, u32[]{:S(2)}) collective-permute-start(bf16[288,2048]{1,0:T(8,128)(2,1)} %collective-permute-done.2), channel_id=1, source_target_pairs={{0,3},{1,0},{4,1},{5,4},{8,5},{9,8},{12,9},{13,12},{14,13},{15,14}... | collective-permute-start | bytes 3538952 | tf_op jit(solution)/shard_map/ppermute | solution.py:149
  57.8 9.4 %copy-start.38 = (s32[16]{0:T(128)S(1)}, s32[16]{0:T(128)}, u32[]{:S(2)}) copy-start(s32[16]{0:T(128)} %constant.102.clone) | copy-start | bytes 196
  57.8 11.1 %copy-start = (s32[16]{0:T(128)S(1)}, s32[16]{0:T(128)}, u32[]{:S(2)}) copy-start(s32[16]{0:T(128)} %constant.103.clone) | copy-start | bytes 196
  60.4 238.7 %all-to-all-start = ((bf16[16,256,288]{1,2,0:T(8,128)(2,1)}), bf16[16,256,288]{1,2,0:T(8,128)(2,1)}, u32[]{:S(2)}, u32[]{:S(2)}) async-start(bf16[16,256,288]{1,2,0:T(8,128)(2,1)} %fusion.110), calls=%async_computation | async-start | bytes 4718592 | tf_op jit(solution)/shard_map/all_to_all | solution.py:211
  68.5 33.5 %collective-permute-start.11 = (bf16[288,2048]{1,0:T(8,128)(2,1)}, bf16[288,2048]{1,0:T(8,128)(2,1)}, u32[]{:S(2)}, u32[]{:S(2)}) collective-permute-start(bf16[288,2048]{1,0:T(8,128)(2,1)} %collective-permute-done.10), channel_id=1, source_target_pairs={{0,1},{1,4},{4,5},{5,8},{8,9},{9,12},{12,13},{13,14},{14,15},{15,1... | collective-permute-start | bytes 3538952 | tf_op jit(solution)/shard_map/ppermute | solution.py:145
  69.6 50.2 %copy-start.27 = (bf16[1,256,2048]{2,1,0:T(8,128)(2,1)S(1)}, bf16[1,256,2048]{2,1,0:T(8,128)(2,1)}, u32[]{:S(2)}) copy-start(bf16[1,256,2048]{2,1,0:T(8,128)(2,1)} %param.14) | copy-start | bytes 3145732
  75.5 53.4 %collective-permute-start.4 = (bf16[288,2048]{1,0:T(8,128)(2,1)}, bf16[288,2048]{1,0:T(8,128)(2,1)}, u32[]{:S(2)}, u32[]{:S(2)}) collective-permute-start(bf16[288,2048]{1,0:T(8,128)(2,1)} %collective-permute-done.3), channel_id=1, source_target_pairs={{0,3},{1,0},{4,1},{5,4},{8,5},{9,8},{12,9},{13,12},{14,13},{15,14}... | collective-permute-start | bytes 3538952 | tf_op jit(solution)/shard_map/ppermute | solution.py:149
  101.9 28.3 %collective-permute-start.12 = (bf16[288,2048]{1,0:T(8,128)(2,1)}, bf16[288,2048]{1,0:T(8,128)(2,1)}, u32[]{:S(2)}, u32[]{:S(2)}) collective-permute-start(bf16[288,2048]{1,0:T(8,128)(2,1)} %collective-permute-done.11), channel_id=1, source_target_pairs={{0,1},{1,4},{4,5},{5,8},{8,9},{9,12},{12,13},{13,14},{14,15},{15,1... | collective-permute-start | bytes 3538952 | tf_op jit(solution)/shard_map/ppermute | solution.py:145
  119.7 7.1 %copy-start.36 = (s32[1024]{0:T(1024)}, s32[1024]{0:T(1024)S(1)}, u32[]{:S(2)}) copy-start(s32[1024]{0:T(1024)S(1)} %pad_clamp_fusion.1) | copy-start | bytes 12292
  128.8 14.1 %collective-permute-start.5 = (bf16[288,2048]{1,0:T(8,128)(2,1)}, bf16[288,2048]{1,0:T(8,128)(2,1)S(1)}, u32[]{:S(2)}, u32[]{:S(2)}) collective-permute-start(bf16[288,2048]{1,0:T(8,128)(2,1)} %collective-permute-done.4), channel_id=1, source_target_pairs={{0,3},{1,0},{4,1},{5,4},{8,5},{9,8},{12,9},{13,12},{14,13},{15,14}... | collective-permute-start | bytes 3538952 | tf_op jit(solution)/shard_map/ppermute | solution.py:149
  130.2 17.1 %collective-permute-start.13 = (bf16[288,2048]{1,0:T(8,128)(2,1)}, bf16[288,2048]{1,0:T(8,128)(2,1)S(1)}, u32[]{:S(2)}, u32[]{:S(2)}) collective-permute-start(bf16[288,2048]{1,0:T(8,128)(2,1)} %collective-permute-done.12), channel_id=1, source_target_pairs={{0,1},{1,4},{4,5},{5,8},{8,9},{9,12},{12,13},{13,14},{14,15},{15,1... | collective-permute-start | bytes 3538952 | tf_op jit(solution)/shard_map/ppermute | solution.py:145
  142.9 18.3 %collective-permute-start.6 = (bf16[288,2048]{1,0:T(8,128)(2,1)S(1)}, bf16[288,2048]{1,0:T(8,128)(2,1)S(1)}, u32[]{:S(2)}, u32[]{:S(2)}) collective-permute-start(bf16[288,2048]{1,0:T(8,128)(2,1)S(1)} %collective-permute-done.5), channel_id=1, source_target_pairs={{0,3},{1,0},{4,1},{5,4},{8,5},{9,8},{12,9},{13,12},{14,13},{15,14}... | collective-permute-start | bytes 3538952 | tf_op jit(solution)/shard_map/ppermute | solution.py:149
  147.4 15.8 %collective-permute-start.14 = (bf16[288,2048]{1,0:T(8,128)(2,1)S(1)}, bf16[288,2048]{1,0:T(8,128)(2,1)S(1)}, u32[]{:S(2)}, u32[]{:S(2)}) collective-permute-start(bf16[288,2048]{1,0:T(8,128)(2,1)S(1)} %collective-permute-done.13), channel_id=1, source_target_pairs={{0,1},{1,4},{4,5},{5,8},{8,9},{9,12},{12,13},{13,14},{14,15},{15,1... | collective-permute-start | bytes 3538952 | tf_op jit(solution)/shard_map/ppermute | solution.py:145
  168.5 6.5 %copy-start.7 = (bf16[16,288,2048]{2,1,0:T(8,128)(2,1)}, bf16[16,288,2048]{2,1,0:T(8,128)(2,1)S(1)}, u32[]{:S(2)}) copy-start(bf16[16,288,2048]{2,1,0:T(8,128)(2,1)S(1)} %bitcast_dynamic-update-slice_fusion) | copy-start | bytes 56623108
  182.9 22.6 %copy-start.3 = (bf16[256,8,128]{2,0,1:T(8,128)(2,1)S(1)}, bf16[256,8,128]{2,0,1:T(8,128)(2,1)}, u32[]{:S(2)}) copy-start(bf16[256,8,128]{2,0,1:T(8,128)(2,1)} %maximum_convert_fusion) | copy-start | bytes 1572868
  182.9 22.6 %copy-start.25 = (pred[256,256]{0,1:T(8,128)(4,1)S(1)}, pred[256,256]{0,1:T(8,128)(4,1)}, u32[]{:S(2)}) copy-start(pred[256,256]{0,1:T(8,128)(4,1)} %fusion.89) | copy-start | bytes 196612
  182.9 36.2 %collective-permute-start.15 = (bf16[256,1024]{0,1:T(8,128)(2,1)}, bf16[256,1024]{0,1:T(8,128)(2,1)S(1)}, u32[]{:S(2)}, u32[]{:S(2)}) collective-permute-start(bf16[256,1024]{0,1:T(8,128)(2,1)} %bitcast.256), channel_id=1, source_target_pairs={{0,2},{2,4},{4,6},{6,8},{8,10},{10,12},{12,14},{1,3},{3,5},{5,7},{... | collective-permute-start | bytes 1572872 | tf_op jit(solution)/shard_map/ppermute | solution.py:22
  199.7 19.3 %collective-permute-start.16 = (bf16[256,1024]{1,0:T(8,128)(2,1)}, bf16[256,1024]{1,0:T(8,128)(2,1)S(1)}, u32[]{:S(2)}, u32[]{:S(2)}) collective-permute-start(bf16[256,1024]{1,0:T(8,128)(2,1)} %fusion.50), channel_id=1, source_target_pairs={{0,2},{2,4},{4,6},{6,8},{8,10},{10,12},{12,14},{1,3},{3,5},{5,7},{... | collective-permute-start | bytes 1572872 | tf_op jit(solution)/shard_map/ppermute | solution.py:22
  205.5 13.6 %copy-start.26 = (pred[256,256]{0,1:T(8,128)(4,1)S(1)}, pred[256,256]{0,1:T(8,128)(4,1)}, u32[]{:S(2)}) copy-start(pred[256,256]{0,1:T(8,128)(4,1)} %fusion.88) | copy-start | bytes 196612
  206.5 19.0 %copy-start.1 = (f32[8,256,256,2]{2,1,3,0:T(8,128)}, f32[8,256,256,2]{2,1,3,0:T(8,128)S(1)}, u32[]{:S(2)}) copy-start(f32[8,256,256,2]{2,1,3,0:T(8,128)S(1)} %get-tuple-element.48) | copy-start | bytes 12582916
  222.3 8.6 %copy-start.33 = (f32[8,2,256]{2,1,0:T(2,128)}, f32[8,2,256]{2,1,0:T(2,128)S(1)}, u32[]{:S(2)}) copy-start(f32[8,2,256]{2,1,0:T(2,128)S(1)} %add.147) | copy-start | bytes 49156
  228.8 18.3 %copy-start.2 = (bf16[8,2,256,256]{2,3,1,0:T(8,128)(2,1)}, bf16[8,2,256,256]{2,3,1,0:T(8,128)(2,1)S(1)}, u32[]{:S(2)}) copy-start(bf16[8,2,256,256]{2,3,1,0:T(8,128)(2,1)S(1)} %get-tuple-element.41) | copy-start | bytes 6291460
  229.6 17.5 %collective-permute-start.17 = (bf16[256,8,128]{2,0,1:T(8,128)(2,1)S(1)}, bf16[256,8,128]{2,0,1:T(8,128)(2,1)S(1)}, u32[]{:S(2)}, u32[]{:S(2)}) collective-permute-start(bf16[256,8,128]{2,0,1:T(8,128)(2,1)S(1)} %fusion.59), channel_id=1, source_target_pairs={{2,0},{4,2},{6,4},{8,6},{10,8},{12,10},{14,12},{3,1},{5,3},{7,5},{... | collective-permute-start | bytes 1572872 | tf_op jit(solution)/shard_map/ppermute | solution.py:22
  233.3 14.5 %copy-start.24 = (f32[256,64]{1,0:T(8,128)S(1)}, f32[256,64]{1,0:T(8,128)}, u32[]{:S(2)}) copy-start(f32[256,64]{1,0:T(8,128)} %get-tuple-element.44) | copy-start | bytes 196612
  233.3 25.1 %collective-permute-start.18 = (bf16[256,8,128]{0,2,1:T(8,128)(2,1)}, bf16[256,8,128]{0,2,1:T(8,128)(2,1)}, u32[]{:S(2)}, u32[]{:S(2)}) collective-permute-start(bf16[256,8,128]{0,2,1:T(8,128)(2,1)} %fusion.60), channel_id=1, source_target_pairs={{2,0},{4,2},{6,4},{8,6},{10,8},{12,10},{14,12},{3,1},{5,3},{7,5},{... | collective-permute-start | bytes 1572872 | tf_op jit(solution)/shard_map/ppermute | solution.py:22
  262.8 35.5 %copy-start.39 = (s32[16]{0:T(128)S(1)}, s32[16]{0:T(128)}, u32[]{:S(2)}) copy-start(s32[16]{0:T(128)} %constant.102.clone) | copy-start | bytes 196
  264.8 38.2 %copy-start.4 = (bf16[256,8,128]{2,0,1:T(8,128)(2,1)S(1)}, bf16[256,8,128]{2,0,1:T(8,128)(2,1)}, u32[]{:S(2)}) copy-start(bf16[256,8,128]{2,0,1:T(8,128)(2,1)} %maximum_convert_fusion) | copy-start | bytes 1572868
  266.2 14.9 %collective-permute-start.26 = (bf16[256,2048]{1,0:T(8,128)(2,1)S(1)}, bf16[256,2048]{1,0:T(8,128)(2,1)S(1)}, u32[]{:S(2)}, u32[]{:S(2)}) collective-permute-start(bf16[256,2048]{1,0:T(8,128)(2,1)S(1)} %pad_maximum_fusion), channel_id=1, source_target_pairs={{0,1},{1,4},{4,5},{5,8},{8,9},{9,12},{12,13},{13,14},{14,15},{15,1... | collective-permute-start | bytes 3145736 | tf_op jit(solution)/shard_map/ppermute | solution.py:145
  266.9 17.1 %collective-permute-start.19 = (bf16[256,2048]{1,0:T(8,128)(2,1)S(1)}, bf16[256,2048]{1,0:T(8,128)(2,1)}, u32[]{:S(2)}, u32[]{:S(2)}) collective-permute-start(bf16[256,2048]{1,0:T(8,128)(2,1)S(1)} %pad_maximum_fusion), channel_id=1, source_target_pairs={{0,3},{1,0},{4,1},{5,4},{8,5},{9,8},{12,9},{13,12},{14,13},{15,14}... | collective-permute-start | bytes 3145736 | tf_op jit(solution)/shard_map/ppermute | solution.py:149
  282.1 14.3 %collective-permute-start.27 = (bf16[256,2048]{1,0:T(8,128)(2,1)S(1)}, bf16[256,2048]{1,0:T(8,128)(2,1)}, u32[]{:S(2)}, u32[]{:S(2)}) collective-permute-start(bf16[256,2048]{1,0:T(8,128)(2,1)S(1)} %collective-permute-done.26), channel_id=1, source_target_pairs={{0,1},{1,4},{4,5},{5,8},{8,9},{9,12},{12,13},{13,14},{14,15},{15,1... | collective-permute-start | bytes 3145736 | tf_op jit(solution)/shard_map/ppermute | solution.py:145
  284.0 21.3 %collective-permute-start.20 = (bf16[256,2048]{1,0:T(8,128)(2,1)}, bf16[256,2048]{1,0:T(8,128)(2,1)}, u32[]{:S(2)}, u32[]{:S(2)}) collective-permute-start(bf16[256,2048]{1,0:T(8,128)(2,1)} %collective-permute-done.19), channel_id=1, source_target_pairs={{0,3},{1,0},{4,1},{5,4},{8,5},{9,8},{12,9},{13,12},{14,13},{15,14}... | collective-permute-start | bytes 3145736 | tf_op jit(solution)/shard_map/ppermute | solution.py:149
  296.4 14.5 %collective-permute-start.28 = (bf16[256,2048]{1,0:T(8,128)(2,1)}, bf16[256,2048]{1,0:T(8,128)(2,1)}, u32[]{:S(2)}, u32[]{:S(2)}) collective-permute-start(bf16[256,2048]{1,0:T(8,128)(2,1)} %collective-permute-done.27), channel_id=1, source_target_pairs={{0,1},{1,4},{4,5},{5,8},{8,9},{9,12},{12,13},{13,14},{14,15},{15,1... | collective-permute-start | bytes 3145736 | tf_op jit(solution)/shard_map/ppermute | solution.py:145
  303.0 9.9 %copy-start.6 = (bf16[8,2,256,256]{2,3,1,0:T(8,128)(2,1)S(1)}, bf16[8,2,256,256]{2,3,1,0:T(8,128)(2,1)}, u32[]{:S(2)}) copy-start(bf16[8,2,256,256]{2,3,1,0:T(8,128)(2,1)} %copy-done.5) | copy-start | bytes 6291460
  303.0 9.9 %copy-start.15 = (bf16[256,1024]{0,1:T(8,128)(2,1)S(1)}, bf16[256,1024]{0,1:T(8,128)(2,1)}, u32[]{:S(2)}) copy-start(bf16[256,1024]{0,1:T(8,128)(2,1)} %copy-done.14) | copy-start | bytes 1572868
  305.3 11.3 %copy-start.31 = (bf16[256,8,128]{0,2,1:T(8,128)(2,1)S(1)}, bf16[256,8,128]{0,2,1:T(8,128)(2,1)}, u32[]{:S(2)}) copy-start(bf16[256,8,128]{0,2,1:T(8,128)(2,1)} %copy-done.30) | copy-start | bytes 1572868
  305.3 16.6 %collective-permute-start.21 = (bf16[256,2048]{1,0:T(8,128)(2,1)}, bf16[256,2048]{1,0:T(8,128)(2,1)}, u32[]{:S(2)}, u32[]{:S(2)}) collective-permute-start(bf16[256,2048]{1,0:T(8,128)(2,1)} %collective-permute-done.20), channel_id=1, source_target_pairs={{0,3},{1,0},{4,1},{5,4},{8,5},{9,8},{12,9},{13,12},{14,13},{15,14}... | collective-permute-start | bytes 3145736 | tf_op jit(solution)/shard_map/ppermute | solution.py:149
  311.0 14.5 %collective-permute-start.29 = (bf16[256,2048]{1,0:T(8,128)(2,1)}, bf16[256,2048]{1,0:T(8,128)(2,1)}, u32[]{:S(2)}, u32[]{:S(2)}) collective-permute-start(bf16[256,2048]{1,0:T(8,128)(2,1)} %collective-permute-done.28), channel_id=1, source_target_pairs={{0,1},{1,4},{4,5},{5,8},{8,9},{9,12},{12,13},{13,14},{14,15},{15,1... | collective-permute-start | bytes 3145736 | tf_op jit(solution)/shard_map/ppermute | solution.py:145
  321.9 35.4 %collective-permute-start.22 = (bf16[256,2048]{1,0:T(8,128)(2,1)}, bf16[256,2048]{1,0:T(8,128)(2,1)}, u32[]{:S(2)}, u32[]{:S(2)}) collective-permute-start(bf16[256,2048]{1,0:T(8,128)(2,1)} %collective-permute-done.21), channel_id=1, source_target_pairs={{0,3},{1,0},{4,1},{5,4},{8,5},{9,8},{12,9},{13,12},{14,13},{15,14}... | collective-permute-start | bytes 3145736 | tf_op jit(solution)/shard_map/ppermute | solution.py:149
  325.5 33.5 %collective-permute-start.30 = (bf16[256,2048]{1,0:T(8,128)(2,1)}, bf16[256,2048]{1,0:T(8,128)(2,1)}, u32[]{:S(2)}, u32[]{:S(2)}) collective-permute-start(bf16[256,2048]{1,0:T(8,128)(2,1)} %collective-permute-done.29), channel_id=1, source_target_pairs={{0,1},{1,4},{4,5},{5,8},{8,9},{9,12},{12,13},{13,14},{14,15},{15,1... | collective-permute-start | bytes 3145736 | tf_op jit(solution)/shard_map/ppermute | solution.py:145
  341.4 17.8 %copy-start.37 = (f32[256]{0:T(256)S(1)}, f32[256]{0:T(256)}, u32[]{:S(2)}) copy-start(f32[256]{0:T(256)} %get-tuple-element.45) | copy-start | bytes 3076
  347.5 23.1 %all-to-all-start.1 = ((f32[16,1,288]{2,1,0:T(1,128)}), f32[16,1,288]{2,1,0:T(1,128)S(1)}, u32[]{:S(2)}, u32[]{:S(2)}) async-start(f32[16,1,288]{2,1,0:T(1,128)} %mul.289), calls=%async_computation.1 | async-start | bytes 49152 | tf_op jit(solution)/shard_map/all_to_all | solution.py:235
  357.3 14.5 %collective-permute-start.23 = (bf16[256,2048]{1,0:T(8,128)(2,1)}, bf16[256,2048]{1,0:T(8,128)(2,1)}, u32[]{:S(2)}, u32[]{:S(2)}) collective-permute-start(bf16[256,2048]{1,0:T(8,128)(2,1)} %collective-permute-done.22), channel_id=1, source_target_pairs={{0,3},{1,0},{4,1},{5,4},{8,5},{9,8},{12,9},{13,12},{14,13},{15,14}... | collective-permute-start | bytes 3145736 | tf_op jit(solution)/shard_map/ppermute | solution.py:149
  359.0 17.2 %collective-permute-start.31 = (bf16[256,2048]{1,0:T(8,128)(2,1)}, bf16[256,2048]{1,0:T(8,128)(2,1)S(1)}, u32[]{:S(2)}, u32[]{:S(2)}) collective-permute-start(bf16[256,2048]{1,0:T(8,128)(2,1)} %collective-permute-done.30), channel_id=1, source_target_pairs={{0,1},{1,4},{4,5},{5,8},{8,9},{9,12},{12,13},{13,14},{14,15},{15,1... | collective-permute-start | bytes 3145736 | tf_op jit(solution)/shard_map/ppermute | solution.py:145
  359.2 6.1 %copy-start.8 = (bf16[256,1024]{1,0:T(8,128)(2,1)S(1)}, bf16[256,1024]{1,0:T(8,128)(2,1)}, u32[]{:S(2)}) copy-start(bf16[256,1024]{1,0:T(8,128)(2,1)} %copy.121) | copy-start | bytes 1572868
  371.8 14.7 %collective-permute-start.24 = (bf16[256,2048]{1,0:T(8,128)(2,1)}, bf16[256,2048]{1,0:T(8,128)(2,1)S(1)}, u32[]{:S(2)}, u32[]{:S(2)}) collective-permute-start(bf16[256,2048]{1,0:T(8,128)(2,1)} %collective-permute-done.23), channel_id=1, source_target_pairs={{0,3},{1,0},{4,1},{5,4},{8,5},{9,8},{12,9},{13,12},{14,13},{15,14}... | collective-permute-start | bytes 3145736 | tf_op jit(solution)/shard_map/ppermute | solution.py:149
  376.2 14.8 %collective-permute-start.32 = (bf16[256,2048]{1,0:T(8,128)(2,1)S(1)}, bf16[256,2048]{1,0:T(8,128)(2,1)S(1)}, u32[]{:S(2)}, u32[]{:S(2)}) collective-permute-start(bf16[256,2048]{1,0:T(8,128)(2,1)S(1)} %collective-permute-done.31), channel_id=1, source_target_pairs={{0,1},{1,4},{4,5},{5,8},{8,9},{9,12},{12,13},{13,14},{14,15},{15,1... | collective-permute-start | bytes 3145736 | tf_op jit(solution)/shard_map/ppermute | solution.py:145
  386.5 14.4 %collective-permute-start.25 = (bf16[256,2048]{1,0:T(8,128)(2,1)S(1)}, bf16[256,2048]{1,0:T(8,128)(2,1)S(1)}, u32[]{:S(2)}, u32[]{:S(2)}) collective-permute-start(bf16[256,2048]{1,0:T(8,128)(2,1)S(1)} %collective-permute-done.24), channel_id=1, source_target_pairs={{0,3},{1,0},{4,1},{5,4},{8,5},{9,8},{12,9},{13,12},{14,13},{15,14}... | collective-permute-start | bytes 3145736 | tf_op jit(solution)/shard_map/ppermute | solution.py:149
  390.9 14.2 %collective-permute-start.33 = (bf16[256,2048]{1,0:T(8,128)(2,1)S(1)}, bf16[256,2048]{1,0:T(8,128)(2,1)S(1)}, u32[]{:S(2)}, u32[]{:S(2)}) collective-permute-start(bf16[256,2048]{1,0:T(8,128)(2,1)S(1)} %collective-permute-done.32), channel_id=1, source_target_pairs={{0,1},{1,4},{4,5},{5,8},{8,9},{9,12},{12,13},{13,14},{14,15},{15,1... | collective-permute-start | bytes 3145736 | tf_op jit(solution)/shard_map/ppermute | solution.py:145
  408.3 9.6 %copy-start.29 = (bf16[256,2048]{1,0:T(8,128)(2,1)S(1)}, bf16[256,2048]{1,0:T(8,128)(2,1)}, u32[]{:S(2)}) copy-start(bf16[256,2048]{1,0:T(8,128)(2,1)} %copy-done.28) | copy-start | bytes 3145732
  410.8 8.2 %copy-start.10 = (bf16[16,256,288]{1,2,0:T(8,128)(2,1)S(1)}, bf16[16,256,288]{1,2,0:T(8,128)(2,1)}, u32[]{:S(2)}) copy-start(bf16[16,256,288]{1,2,0:T(8,128)(2,1)} %gather_fusion.3) | copy-start | bytes 7077892
  410.8 8.2 %copy-start.41 = (pred[16]{0:T(512)(128)(4,1)S(1)}, pred[16]{0:T(512)(128)(4,1)}, u32[]{:S(2)}) copy-start(pred[16]{0:T(512)(128)(4,1)} %compare_and_fusion) | copy-start | bytes 52
  (14 other events, 46.1 us)
